TPU v7x, 32 devices: a whole 2x2x4 slice. The times are simulated.
32 devices in a mesh: tensor: 2 (over y), req: 4 (over z), seq: 4 (over x, core).
Axes of the slice: x: 2, y: 2, z: 4, core: 2. Of those that a mesh axis runs over, the one named last changes fastest.
Arguments:
- draft_query: bfloat16 [4, 64, 8192], P('req', None, 'tensor'), may hold values from -6 to 6
- draft_kv: bfloat16 [4, 2, 64, 1024], P('req', None, None, 'tensor'), may hold values from -6 to 6
- own_cache: bfloat16 [4, 2, 32768, 1024], P('req', None, 'seq', 'tensor'), may hold values from -6 to 6
- shared_cache: bfloat16 [2, 2, 8192, 1024], P(None, None, ('req', 'seq'), 'tensor'), may hold values from -6 to 6
- out_weight: bfloat16 [8192, 8192], P(('tensor', 'seq')), may hold values from -0.09375 to 0.09375
- lengths: int32 [4], P('req'), may hold values from 1 to 32768, as said below
- group_ids: int32 [4], replicated, may hold values from 0 to 1
- parents: int32 [4, 64], P('req'), may hold values from -1 to 62, as said below
- accepted: int32 [4, 8], P('req'), may hold values from 0 to 62, as said below
Outputs:
- verified: bfloat16 [4, 64, 8192], P('req', None, ('tensor', 'seq'))
- accepted_kv: bfloat16 [4, 2, 8, 1024], P('req', None, None, 'tensor')
Inputs may be any that keep to these rules, and one draw needn't show every extreme that they name: Request r attends to own cache positions 0 to lengths[r] - 1; some request has exactly 32768. parents[r, 0] = -1 and 0 <= parents[r, i] < i for i >= 1. accepted[r, 0] = 0 and parents[r, accepted[r, a]] = accepted[r, a - 1]: a path from the root.
All inputs are finite; a program needn't handle non-finite values.
Results may differ from a plain program's by a relative error of at most 0.012.
Values may be sent and summed in bfloat16 or wider, within the bound.
No kernel may reach another device: no remote copies, remote signals or barrier semaphores. Data moves between devices by JAX's collectives and lax.ppermute only.
A program may use at most 192 MiB of HBM per device.

v0:
```python
import jax
import jax.numpy as jnp
from jax import lax
from jax.sharding import PartitionSpec as P

HD = 128
QPK = 8


NEG_FILL = -1e30


def merged(value, axis, join):
    pieces = jax.tree.map(lambda part: lax.all_gather(part, axis), value)
    head = jax.tree.map(lambda part: part[0], pieces)
    tail = jax.tree.map(lambda part: part[1:], pieces)
    subtotal, _ = lax.scan(lambda subtotal, slab: (join(subtotal, slab), None), head, tail)
    return subtotal


def combine(first, second):
    first_max, first_total, first_sum = first
    second_max, second_total, second_sum = second
    joined = jnp.maximum(first_max, second_max)
    first_factor = jnp.exp(first_max - joined)
    second_factor = jnp.exp(second_max - joined)
    return (
        joined,
        first_total * first_factor + second_total * second_factor,
        first_sum * first_factor[..., None] + second_sum * second_factor[..., None],
    )


def update(state, queries, key_block, value_block, valid):
    run_max, run_total, run_sum = state
    scores = jnp.einsum(
        "hrd,khd->hrk", queries, key_block, preferred_element_type=jnp.float32
    ) * HD ** (-0.5)
    if valid is not None:
        scores = jnp.where(valid[None, None, :], scores, NEG_FILL)
    new_max = jnp.maximum(run_max, jnp.max(scores, axis=2))
    weights = jnp.exp(scores - new_max[..., None])
    if valid is not None:
        weights = jnp.where(valid[None, None, :], weights, 0.0)
    factor = jnp.exp(run_max - new_max)
    run_total = run_total * factor + jnp.sum(weights, axis=2)
    run_sum = run_sum * factor[..., None] + jnp.einsum(
        "hrk,khd->hrd",
        weights.astype(jnp.bfloat16),
        value_block,
        preferred_element_type=jnp.float32,
    )
    return (new_max, run_total, run_sum)


def tree_reach(parent_row):
    node_count = parent_row.shape[0]
    nodes = jnp.arange(node_count, dtype=jnp.int32)
    reach = jnp.eye(node_count, dtype=jnp.float32) + (parent_row[:, None] == nodes[None, :]).astype(
        jnp.float32
    )
    for level_step in range(max(node_count - 1, 1).bit_length()):
        reach = jnp.minimum(jnp.dot(reach, reach, precision=lax.Precision.HIGHEST), 1.0)
    return reach > 0.5


def shards(
    draft_query,
    draft_kv,
    own_cache,
    shared_cache,
    out_weight,
    lengths,
    group_ids,
    parents,
    accepted,
):
    kv_heads = own_cache.shape[3] // HD
    draft_len = draft_query.shape[1]
    query_rows = QPK * draft_len
    seq_count = lax.axis_size("seq")
    seq_index = lax.axis_index("seq")
    req_index = lax.axis_index("req")
    queries = (
        draft_query[0]
        .reshape(draft_len, kv_heads, QPK, HD)
        .transpose(1, 2, 0, 3)
        .reshape(kv_heads, query_rows, HD)
    )
    state = (
        jnp.full((kv_heads, query_rows), NEG_FILL, jnp.float32),
        jnp.zeros((kv_heads, query_rows), jnp.float32),
        jnp.zeros((kv_heads, query_rows, HD), jnp.float32),
    )
    cache_len = own_cache.shape[2]
    block_len = min(2048, cache_len)
    own_length = lengths[0]

    def own_step(running, block_index):
        first_row = block_index * block_len
        block = lax.dynamic_slice_in_dim(own_cache[0], first_row, block_len, 1)
        positions = seq_index * cache_len + first_row + jnp.arange(block_len, dtype=jnp.int32)
        valid = positions < own_length
        return (
            update(
                running,
                queries,
                block[0].reshape(block_len, kv_heads, HD),
                block[1].reshape(block_len, kv_heads, HD),
                valid,
            ),
            None,
        )

    state, unused = lax.scan(own_step, state, jnp.arange(cache_len // block_len, dtype=jnp.int32))
    own_group = group_ids[req_index]
    selected = lax.dynamic_index_in_dim(
        lax.all_gather(shared_cache, "req", axis=2, tiled=True), own_group, 1, keepdims=False
    )
    piece_len = selected.shape[1]
    state = update(
        state,
        queries,
        selected[0].reshape(piece_len, kv_heads, HD),
        selected[1].reshape(piece_len, kv_heads, HD),
        None,
    )
    heads_dev = kv_heads * QPK
    head_share = heads_dev // seq_count
    flat_max = state[0].reshape(heads_dev, draft_len)
    flat_total = state[1].reshape(heads_dev, draft_len)
    flat_sum = state[2].reshape(heads_dev, draft_len, HD)
    combined = merged((flat_max, flat_total, flat_sum), "seq", combine)
    own_heads = tuple(
        (
            lax.dynamic_slice_in_dim(member, seq_index * head_share, head_share, 0)
            for member in combined
        )
    )
    reach = tree_reach(parents[0])
    head_queries = lax.dynamic_slice_in_dim(
        draft_query[0], seq_index * head_share * HD, head_share * HD, 1
    )
    head_queries = head_queries.reshape(draft_len, head_share, HD)
    kv_select = (seq_index * head_share + jnp.arange(head_share, dtype=jnp.int32)) // QPK
    draft_keys = jnp.take(draft_kv[0, 0].reshape(draft_len, kv_heads, HD), kv_select, axis=1)
    draft_values = jnp.take(draft_kv[0, 1].reshape(draft_len, kv_heads, HD), kv_select, axis=1)
    tree_scores = jnp.einsum(
        "thd,uhd->htu", head_queries, draft_keys, preferred_element_type=jnp.float32
    ) * HD ** (-0.5)
    tree_scores = jnp.where(reach[None], tree_scores, NEG_FILL)
    tree_max = jnp.max(tree_scores, axis=2)
    tree_weights = jnp.where(reach[None], jnp.exp(tree_scores - tree_max[..., None]), 0.0)
    tree_part = (
        tree_max,
        jnp.sum(tree_weights, axis=2),
        jnp.einsum(
            "htu,uhd->htd",
            tree_weights.astype(jnp.bfloat16),
            draft_values,
            preferred_element_type=jnp.float32,
        ),
    )
    final_max, final_total, final_sum = combine(own_heads, tree_part)
    attended = (final_sum / final_total[..., None]).astype(jnp.bfloat16)
    attended = jnp.transpose(attended, (1, 0, 2)).reshape(draft_len, head_share * HD)
    out_piece = lax.psum_scatter(
        lax.dot_general(
            out_weight, attended, (((0,), (1,)), ((), ())), preferred_element_type=jnp.float32
        ),
        ("tensor", "seq"),
        scatter_dimension=0,
        tiled=True,
    )
    verified = out_piece.T[None].astype(jnp.bfloat16)
    accepted_kv = jnp.take(draft_kv[0], accepted[0], axis=1)[None]
    return (verified, accepted_kv)


def solution(mesh):
    placed = (
        P("req", None, "tensor"),
        P("req", None, None, "tensor"),
        P("req", None, "seq", "tensor"),
        P(None, None, ("req", "seq"), "tensor"),
        P(("tensor", "seq"), None),
        P("req"),
        P(),
        P("req", None),
        P("req", None),
    )
    return jax.shard_map(
        shards,
        mesh=mesh,
        in_specs=placed,
        out_specs=(P("req", None, ("tensor", "seq")), P("req", None, None, "tensor")),
        check_vma=False,
    )
```

profile of v0, /device:TPU:8, one launch (start us, length us, event | category | flops | bytes accessed | tf_op | source)
XLA Modules:
  0.0 317.4 jit_solution(569340358236294364)
XLA Ops:
  7.2 4.2 %copy.53 = bf16[2,2,512,512]{2,3,1,0:T(8,128)(2,1)} copy(bf16[2,2,512,512]{3,2,1,0:T(8,128)(2,1)} %param.18) | data formatting | bytes 4194304 | tf_op args[3]
  11.5 1.1 copy.76
  12.6 0.2 copy.51
  12.9 1.3 dynamic_slice.39
  16.0 162.9 %while.32 = (s32[]{:T(128)}, f32[4,512]{1,0:T(4,128)S(1)}, f32[4,512]{1,0:T(4,128)S(1)}, f32[4,512,128]{2,1,0:T(8,128)}, s32[4]{0:T(128)S(1)}, /*index=5*/s32[]{...) while((s32[]{:T(128)}, f32[4,512]{1,0:T(4,128)S(1)}, ...), condition=%wide.region_3.4_spmd.clone, body=%wide.region_0.3_spmd.clone.sunk | while | flops 2202810368 | bytes 74064120 | solution.py:115
  16.1 0.6 dynamic_slice.65
  17.3 0.7 add_compare_fusion.2
  18.0 4.2 %constant_dynamic-slice_fusion.5 = (bf16[1,1,2048,512]{3,2,1,0:T(8,128)(2,1)S(1)}, bf16[1,1,2048,512]{3,2,1,0:T(8,128)(2,1)}) fusion(bf16[1,2,8192,512]{3,2,1,0:T(8,128)(2,1)} %get-tuple-element.428, s32[]{:T(128)S(6)} %add.181, s32[]{:T(128)S(6)} %select_n.163), kind=kLoop, calls=%fused_computation.29.clone.1 | loop fusion | bytes 8388616 | tf_op jit(solution)/shard_map/while/body/eval_jaxpr/slice | solution.py:109
  22.1 4.1 %copy.90 = bf16[1,1,2048,512]{2,3,1,0:T(8,128)(2,1)} copy(bf16[1,1,2048,512]{3,2,1,0:T(8,128)(2,1)} %get-tuple-element.387) | data formatting | bytes 4194304 | tf_op jit(solution)/shard_map/while
  26.2 9.0 %bitcast_reduce_fusion.3 = (f32[4,512]{1,0:T(4,128)S(1)}, f32[4,2048,512]{2,1,0:T(8,128)}) fusion(pred[2048]{0:T(1024)(128)(4,1)S(1)} %add_compare_fusion.2, bf16[2048,4,128]{0,2,1:T(8,128)(2,1)} %bitcast.143, bf16[4,512,128]{2,1,0:T(8,128)(2,1)S(1)} %get-tuple-element.429), kind=kOutput, calls=%fused_computation.12.clone.1 | convolution fusion | flops 1086322688 | bytes 19408896 | tf_op jit(solution)/shard_map/while/body/eval_jaxpr/hrd,khd->hrk/dot_general | solution.py:36
  35.2 8.3 %fusion.99 = f32[4,512]{1,0:T(4,128)S(1)} fusion(f32[4,2048,512]{2,1,0:T(8,128)} %get-tuple-element.389, f32[4,512]{1,0:T(4,128)S(1)} %select_maximum_fusion.2, pred[2048]{0:T(1024)(128)(4,1)S(1)} %add_compare_fusion.2), kind=kLoop, calls=%fused_computation.17.clone.1 | loop fusion | flops 20969472 | bytes 16795648 | tf_op jit(solution)/shard_map/while/body/eval_jaxpr/reduce_sum | solution.py:46
  43.5 2.4 copy.91
  46.0 11.1 %fusion.101 = f32[4,512,128]{2,1,0:T(8,128)} fusion(bf16[2048,4,128]{0,2,1:T(8,128)(2,1)} %bitcast.144, f32[4,2048,512]{2,1,0:T(8,128)} %get-tuple-element.389, f32[4,512]{1,0:T(4,128)S(1)} %select_maximum_fusion.2, pred[2048]{0:T(1024)(128)(4,1)S(1)} %add_compare_fusion.2, f32[4,512,128]{2,1,0:T(8,128)} %get-tuple-element.410, ...), kind=kOutput, calls=%fused_computation.21.clone.1 | convolution fusion | flops 1095499776 | bytes 20989952 | tf_op jit(solution)/shard_map/while/body/eval_jaxpr/hrk,khd->hrd/dot_general | solution.py:47
  57.0 0.6 dynamic_slice.65
  58.3 0.7 add_compare_fusion.2
  58.9 3.9 %constant_dynamic-slice_fusion.5 = (bf16[1,1,2048,512]{3,2,1,0:T(8,128)(2,1)S(1)}, bf16[1,1,2048,512]{3,2,1,0:T(8,128)(2,1)}) fusion(bf16[1,2,8192,512]{3,2,1,0:T(8,128)(2,1)} %get-tuple-element.428, s32[]{:T(128)S(6)} %add.181, s32[]{:T(128)S(6)} %select_n.163), kind=kLoop, calls=%fused_computation.29.clone.1 | loop fusion | bytes 8388616 | tf_op jit(solution)/shard_map/while/body/eval_jaxpr/slice | solution.py:109
  62.8 3.9 %copy.90 = bf16[1,1,2048,512]{2,3,1,0:T(8,128)(2,1)} copy(bf16[1,1,2048,512]{3,2,1,0:T(8,128)(2,1)} %get-tuple-element.387) | data formatting | bytes 4194304 | tf_op jit(solution)/shard_map/while
  66.7 8.9 %bitcast_reduce_fusion.3 = (f32[4,512]{1,0:T(4,128)S(1)}, f32[4,2048,512]{2,1,0:T(8,128)}) fusion(pred[2048]{0:T(1024)(128)(4,1)S(1)} %add_compare_fusion.2, bf16[2048,4,128]{0,2,1:T(8,128)(2,1)} %bitcast.143, bf16[4,512,128]{2,1,0:T(8,128)(2,1)S(1)} %get-tuple-element.429), kind=kOutput, calls=%fused_computation.12.clone.1 | convolution fusion | flops 1086322688 | bytes 19408896 | tf_op jit(solution)/shard_map/while/body/eval_jaxpr/hrd,khd->hrk/dot_general | solution.py:36
  75.6 8.3 %fusion.99 = f32[4,512]{1,0:T(4,128)S(1)} fusion(f32[4,2048,512]{2,1,0:T(8,128)} %get-tuple-element.389, f32[4,512]{1,0:T(4,128)S(1)} %select_maximum_fusion.2, pred[2048]{0:T(1024)(128)(4,1)S(1)} %add_compare_fusion.2), kind=kLoop, calls=%fused_computation.17.clone.1 | loop fusion | flops 20969472 | bytes 16795648 | tf_op jit(solution)/shard_map/while/body/eval_jaxpr/reduce_sum | solution.py:46
  84.0 2.4 copy.91
  86.4 11.3 %fusion.101 = f32[4,512,128]{2,1,0:T(8,128)} fusion(bf16[2048,4,128]{0,2,1:T(8,128)(2,1)} %bitcast.144, f32[4,2048,512]{2,1,0:T(8,128)} %get-tuple-element.389, f32[4,512]{1,0:T(4,128)S(1)} %select_maximum_fusion.2, pred[2048]{0:T(1024)(128)(4,1)S(1)} %add_compare_fusion.2, f32[4,512,128]{2,1,0:T(8,128)} %get-tuple-element.410, ...), kind=kOutput, calls=%fused_computation.21.clone.1 | convolution fusion | flops 1095499776 | bytes 20989952 | tf_op jit(solution)/shard_map/while/body/eval_jaxpr/hrk,khd->hrd/dot_general | solution.py:47
  97.7 0.6 dynamic_slice.65
  99.0 0.7 add_compare_fusion.2
  99.6 3.9 %constant_dynamic-slice_fusion.5 = (bf16[1,1,2048,512]{3,2,1,0:T(8,128)(2,1)S(1)}, bf16[1,1,2048,512]{3,2,1,0:T(8,128)(2,1)}) fusion(bf16[1,2,8192,512]{3,2,1,0:T(8,128)(2,1)} %get-tuple-element.428, s32[]{:T(128)S(6)} %add.181, s32[]{:T(128)S(6)} %select_n.163), kind=kLoop, calls=%fused_computation.29.clone.1 | loop fusion | bytes 8388616 | tf_op jit(solution)/shard_map/while/body/eval_jaxpr/slice | solution.py:109
  103.5 3.9 %copy.90 = bf16[1,1,2048,512]{2,3,1,0:T(8,128)(2,1)} copy(bf16[1,1,2048,512]{3,2,1,0:T(8,128)(2,1)} %get-tuple-element.387) | data formatting | bytes 4194304 | tf_op jit(solution)/shard_map/while
  107.4 9.0 %bitcast_reduce_fusion.3 = (f32[4,512]{1,0:T(4,128)S(1)}, f32[4,2048,512]{2,1,0:T(8,128)}) fusion(pred[2048]{0:T(1024)(128)(4,1)S(1)} %add_compare_fusion.2, bf16[2048,4,128]{0,2,1:T(8,128)(2,1)} %bitcast.143, bf16[4,512,128]{2,1,0:T(8,128)(2,1)S(1)} %get-tuple-element.429), kind=kOutput, calls=%fused_computation.12.clone.1 | convolution fusion | flops 1086322688 | bytes 19408896 | tf_op jit(solution)/shard_map/while/body/eval_jaxpr/hrd,khd->hrk/dot_general | solution.py:36
  116.4 8.2 %fusion.99 = f32[4,512]{1,0:T(4,128)S(1)} fusion(f32[4,2048,512]{2,1,0:T(8,128)} %get-tuple-element.389, f32[4,512]{1,0:T(4,128)S(1)} %select_maximum_fusion.2, pred[2048]{0:T(1024)(128)(4,1)S(1)} %add_compare_fusion.2), kind=kLoop, calls=%fused_computation.17.clone.1 | loop fusion | flops 20969472 | bytes 16795648 | tf_op jit(solution)/shard_map/while/body/eval_jaxpr/reduce_sum | solution.py:46
  124.7 2.4 copy.91
  127.1 11.3 %fusion.101 = f32[4,512,128]{2,1,0:T(8,128)} fusion(bf16[2048,4,128]{0,2,1:T(8,128)(2,1)} %bitcast.144, f32[4,2048,512]{2,1,0:T(8,128)} %get-tuple-element.389, f32[4,512]{1,0:T(4,128)S(1)} %select_maximum_fusion.2, pred[2048]{0:T(1024)(128)(4,1)S(1)} %add_compare_fusion.2, f32[4,512,128]{2,1,0:T(8,128)} %get-tuple-element.410, ...), kind=kOutput, calls=%fused_computation.21.clone.1 | convolution fusion | flops 1095499776 | bytes 20989952 | tf_op jit(solution)/shard_map/while/body/eval_jaxpr/hrk,khd->hrd/dot_general | solution.py:47
  138.4 0.6 dynamic_slice.65
  139.7 0.7 add_compare_fusion.2
  140.3 3.8 %constant_dynamic-slice_fusion.5 = (bf16[1,1,2048,512]{3,2,1,0:T(8,128)(2,1)S(1)}, bf16[1,1,2048,512]{3,2,1,0:T(8,128)(2,1)}) fusion(bf16[1,2,8192,512]{3,2,1,0:T(8,128)(2,1)} %get-tuple-element.428, s32[]{:T(128)S(6)} %add.181, s32[]{:T(128)S(6)} %select_n.163), kind=kLoop, calls=%fused_computation.29.clone.1 | loop fusion | bytes 8388616 | tf_op jit(solution)/shard_map/while/body/eval_jaxpr/slice | solution.py:109
  144.1 3.9 %copy.90 = bf16[1,1,2048,512]{2,3,1,0:T(8,128)(2,1)} copy(bf16[1,1,2048,512]{3,2,1,0:T(8,128)(2,1)} %get-tuple-element.387) | data formatting | bytes 4194304 | tf_op jit(solution)/shard_map/while
  148.1 8.9 %bitcast_reduce_fusion.3 = (f32[4,512]{1,0:T(4,128)S(1)}, f32[4,2048,512]{2,1,0:T(8,128)}) fusion(pred[2048]{0:T(1024)(128)(4,1)S(1)} %add_compare_fusion.2, bf16[2048,4,128]{0,2,1:T(8,128)(2,1)} %bitcast.143, bf16[4,512,128]{2,1,0:T(8,128)(2,1)S(1)} %get-tuple-element.429), kind=kOutput, calls=%fused_computation.12.clone.1 | convolution fusion | flops 1086322688 | bytes 19408896 | tf_op jit(solution)/shard_map/while/body/eval_jaxpr/hrd,khd->hrk/dot_general | solution.py:36
  157.0 8.2 %fusion.99 = f32[4,512]{1,0:T(4,128)S(1)} fusion(f32[4,2048,512]{2,1,0:T(8,128)} %get-tuple-element.389, f32[4,512]{1,0:T(4,128)S(1)} %select_maximum_fusion.2, pred[2048]{0:T(1024)(128)(4,1)S(1)} %add_compare_fusion.2), kind=kLoop, calls=%fused_computation.17.clone.1 | loop fusion | flops 20969472 | bytes 16795648 | tf_op jit(solution)/shard_map/while/body/eval_jaxpr/reduce_sum | solution.py:46
  165.2 2.4 copy.91
  167.6 11.3 %fusion.101 = f32[4,512,128]{2,1,0:T(8,128)} fusion(bf16[2048,4,128]{0,2,1:T(8,128)(2,1)} %bitcast.144, f32[4,2048,512]{2,1,0:T(8,128)} %get-tuple-element.389, f32[4,512]{1,0:T(4,128)S(1)} %select_maximum_fusion.2, pred[2048]{0:T(1024)(128)(4,1)S(1)} %add_compare_fusion.2, f32[4,512,128]{2,1,0:T(8,128)} %get-tuple-element.410, ...), kind=kOutput, calls=%fused_computation.21.clone.1 | convolution fusion | flops 1095499776 | bytes 20989952 | tf_op jit(solution)/shard_map/while/body/eval_jaxpr/hrk,khd->hrd/dot_general | solution.py:47
  178.9 2.6 constant_dynamic-slice_fusion.3
  181.6 8.1 %bitcast_reduce_fusion.1 = (f32[4,512]{1,0:T(4,128)S(1)}, f32[4,2048,512]{2,1,0:T(8,128)}) fusion(bf16[2048,4,128]{0,2,1:T(8,128)(2,1)S(1)} %bitcast.146, bf16[4,512,128]{2,1,0:T(8,128)(2,1)S(1)} %get-tuple-element.462), kind=kOutput, calls=%fused_computation.34 | convolution fusion | flops 1082128384 | bytes 19406848 | tf_op jit(solution)/shard_map/hrd,khd->hrk/dot_general | solution.py:36
  189.7 8.6 %fusion.20 = f32[4,512]{1,0:T(4,128)S(1)} fusion(f32[4,2048,512]{2,1,0:T(8,128)} %get-tuple-element.270, f32[4,512]{1,0:T(4,128)S(1)} %max.14), kind=kLoop, calls=%fused_computation.37 | loop fusion | flops 12580864 | bytes 16793600 | tf_op jit(solution)/shard_map/reduce_sum | solution.py:46
  198.4 10.8 %fusion.25 = f32[4,512,128]{2,1,0:T(8,128)} fusion(bf16[2048,4,128]{0,2,1:T(8,128)(2,1)S(1)} %bitcast.147, f32[4,2048,512]{2,1,0:T(8,128)} %get-tuple-element.270, f32[4,512]{1,0:T(4,128)S(1)} %max.14, f32[4,512,128]{2,1,0:T(8,128)} %get-tuple-element.151, f32[4,512]{1,0:T(4,128)S(1)} %get-tuple-element.260), kind=kOutput, calls=%fused_computation.42 | convolution fusion | flops 1086849024 | bytes 20987904 | tf_op jit(solution)/shard_map/hrk,khd->hrd/dot_general | solution.py:47
  209.4 0.9 dynamic-slice_bitcast_fusion
  210.3 0.2 convolution_minimum_fusion.5
  210.6 0.2 convolution_minimum_fusion.4
  210.7 0.2 convolution_minimum_fusion.3
  211.2 0.2 fusion.33
  211.6 0.6 gather_fusion.1
  212.2 0.6 gather_fusion.2
  212.8 0.3 fusion.66
  213.3 5.2 %all_gather.13 = f32[4,32,64]{2,1,0:T(8,128)S(1)} all-gather(f32[1,32,64]{2,1,0:T(8,128)S(1)} %all_gather_reshape.9), channel_id=1, replica_groups=mesh['tensor'=2,'req'=4,'seq'=4] {'seq'}, dimensions={0}, use_global_device_ids=true | all-gather | bytes 40960 | tf_op jit(solution)/shard_map/all_gather | solution.py:14
  218.5 5.6 %all_gather.14 = f32[4,32,64]{2,1,0:T(8,128)S(1)} all-gather(f32[1,32,64]{2,1,0:T(8,128)S(1)} %all_gather_reshape.10), channel_id=1, replica_groups=mesh['tensor'=2,'req'=4,'seq'=4] {'seq'}, dimensions={0}, use_global_device_ids=true | all-gather | bytes 40960 | tf_op jit(solution)/shard_map/all_gather | solution.py:14
  224.2 21.3 %all-gather.5.cloned.1.call-done = f32[4,32,64,128]{3,2,1,0:T(8,128)} async-done(((f32[1,32,64,128]{3,2,1,0:T(8,128)}), f32[4,32,64,128]{3,2,1,0:T(8,128)}) %all-gather.5.cloned.1.call-update) | async-done | bytes 4194320 | tf_op jit(solution)/shard_map/all_gather | solution.py:14
  245.4 1.3 slice_bitcast_fusion
  246.7 4.0 %slice.67 = f32[3,32,64,128]{3,2,1,0:T(8,128)} slice(f32[4,32,64,128]{3,2,1,0:T(8,128)} %all-gather.5.cloned.1.call-done), slice={[1:4], [0:32], [0:64], [0:128]} | slice | bytes 6291456 | tf_op jit(solution)/shard_map/slice | solution.py:16
  250.7 6.7 %while.31 = (s32[]{:T(128)}, f32[32,64]{1,0:T(8,128)S(1)}, f32[32,64]{1,0:T(8,128)S(1)}, f32[32,64,128]{2,1,0:T(8,128)S(1)}, f32[3,32,64]{2,1,0:T(8,128)S(1)}, /...) while((s32[]{:T(128)}, f32[32,64]{1,0:T(8,128)S(1)}, f32[32,64]{1,0:T(8,128)S(1)}, ...), condition=%wide.region_7.8_spmd, body=%wide.region_6.7_spmd.sunk | while | flops 798722 | bytes 3227749 | solution.py:17
  250.7 2.2 fusion.94
  253.0 2.2 fusion.94
  255.2 2.2 fusion.94
  257.4 0.4 fusion.32
  257.8 10.1 %convolution_bitcast_fusion = f32[8192,64]{0,1:T(8,128)} fusion(bf16[1024,8192]{1,0:T(8,128)(2,1)} %param.19, bf16[8,8,8,128]{3,2,1,0:T(8,128)(2,1)S(1)} %fusion.32), kind=kOutput, calls=%fused_computation.38 | convolution fusion | flops 1073741824 | bytes 19005440 | tf_op jit(solution)/shard_map/dot_general | solution.py:168
  268.2 0.6 gather_fusion
  268.8 0.6 copy.64
  269.4 39.8 %reduce-scatter.2.cloned.1.call-done = f32[1024,64]{0,1:T(8,128)} async-done(((f32[8192,64]{0,1:T(8,128)}), f32[1024,64]{0,1:T(8,128)}) %reduce-scatter.2.cloned.1.call-update) | async-done | bytes 262160 | tf_op jit(solution)/shard_map/reduce_scatter | solution.py:167
  309.3 1.6 convert_bitcast_fusion
  (58 shorter events, 1.4 us)
Async XLA Ops:
  7.2 171.8 %all-gather.3.cloned.1.call-start = ((), (), s32[]{:S(2)}) async-start(), calls=%async_computation.1 | async-start | bytes 10485760 | tf_op jit(solution)/shard_map/all_gather | solution.py:118
  11.4 234.0 %all-gather.5.cloned.1.call-start = ((), (), s32[]{:S(2)}) async-start(), calls=%async_computation.2 | async-start | bytes 5242880 | tf_op jit(solution)/shard_map/all_gather | solution.py:14
  189.7 19.6 %copy-start = (bf16[1,2,64,512]{3,2,1,0:T(8,128)(2,1)S(1)}, bf16[1,2,64,512]{3,2,1,0:T(8,128)(2,1)}, u32[]{:S(2)}) copy-start(bf16[1,2,64,512]{3,2,1,0:T(8,128)(2,1)} %param.16) | copy-start | bytes 393220
  189.7 20.6 %copy-start.2 = (s32[1,64]{1,0:T(1,128)S(1)}, s32[1,64]{1,0:T(1,128)}, u32[]{:S(2)}) copy-start(s32[1,64]{1,0:T(1,128)} %param.22) | copy-start | bytes 772
  189.7 23.0 %copy-start.1 = (s32[1,8]{1,0:T(1,128)S(1)}, s32[1,8]{1,0:T(1,128)}, u32[]{:S(2)}) copy-start(s32[1,8]{1,0:T(1,128)} %param.23) | copy-start | bytes 100
  209.2 100.0 %reduce-scatter.2.cloned.1.call-start = ((), (), s32[]{:S(2)}) async-start(), calls=%async_computation.3 | async-start | bytes 2359296 | tf_op jit(solution)/shard_map/reduce_scatter | solution.py:167
Sparse Core Ops, SparseCore 0:
  11.5 147.8 all-gather.2
  209.3 36.0 all-gather.4
  268.1 41.1 reduce-scatter.1
where the time goes:
time: 320 us; the launch traced here: 317 us
  matrix products  112 us (35%)
  local copies, waits for them, and re-layouts  62.2 us (19%)
  waiting for transfers between devices  61.1 us (19%)
  other arithmetic  52.8 us (16%)
  between operations  16 us (5%)
  blocking collectives  10.9 us (3%)
    dot_general x5, matrix products, update(): jnp.einsum('hrk,khd->hrd', weights.astype(jnp.bfloat16), value_block, pre...  55.8 us
    dot_general x5, matrix products, update(): jnp.einsum('hrd,khd->hrk', queries, key_block, preferred_element_type=jnp...  43.9 us
    reduce_sum x5, other arithmetic, update(): run_total = run_total * factor + jnp.sum(weights, axis=2)  41.6 us
    reduce_scatter x1, waiting for transfers between devices, shards(): lax.psum_scatter(lax.dot_general(out_weight, attended, (((0,), (1,)), (()...  39.8 us
    while x12, local copies, waits for them, and re-layouts  25.5 us
    all_gather x1, waiting for transfers between devices, merged(): pieces = jax.tree.map(lambda part: lax.all_gather(part, axis), value)  21.3 us
    slice x4, local copies, waits for them, and re-layouts, own_step(): block[1].reshape(block_len, kv_heads, HD)  15.7 us
    all_gather x2, blocking collectives, merged(): pieces = jax.tree.map(lambda part: lax.all_gather(part, axis), value)  10.9 us
  transfers between devices with their start and end apart: 3, of which 2 were waited for; matrix products, arithmetic and copies ran while one was open for 53% of the time, Pallas kernels for 0%

commit v1 on v0

v1 whole, which is shorter than its diff:
```python
import functools

import jax
import jax.numpy as jnp
from jax import lax
from jax.experimental import pallas as pl
from jax.experimental.pallas import tpu as pltpu
from jax.sharding import PartitionSpec as P

HD = 128
QPK = 8
NEG_FILL = -1e30
SCALE = HD ** (-0.5)
OWN_BLOCK = 512


def step(m_prev, l_prev, acc_prev, q, k, v, ok):
    scores = lax.dot_general(
        q, k, (((1,), (1,)), ((), ())), preferred_element_type=jnp.float32
    ) * SCALE
    if ok is not None:
        scores = jnp.where(ok, scores, NEG_FILL)
    m_new = jnp.maximum(m_prev, jnp.max(scores, axis=1, keepdims=True))
    alpha = jnp.exp(m_prev - m_new)
    weights = jnp.exp(scores - m_new)
    if ok is not None:
        weights = jnp.where(ok, weights, 0.0)
    l_new = alpha * l_prev + jnp.sum(weights, axis=1, keepdims=True)
    acc_new = alpha * acc_prev + jnp.dot(
        weights.astype(jnp.bfloat16), v, preferred_element_type=jnp.float32
    )
    return m_new, l_new, acc_new


def own_kernel(kv_heads, block, nv_ref, q_ref, kv_ref, m_out, l_out, acc_out, m_s, l_s, acc_s):
    j = pl.program_id(0)
    n_valid = nv_ref[0]

    @pl.when(j == 0)
    def _():
        m_s[...] = jnp.full(m_s.shape, NEG_FILL, jnp.float32)
        l_s[...] = jnp.zeros(l_s.shape, jnp.float32)
        acc_s[...] = jnp.zeros(acc_s.shape, jnp.float32)

    start = j * block

    def body(masked):
        ok = None
        if masked:
            cols = start + lax.broadcasted_iota(jnp.int32, (1, block), 1)
            ok = cols < n_valid
        for h in range(kv_heads):
            cols_h = slice(h * HD, (h + 1) * HD)
            m, l, acc = step(
                m_s[h], l_s[h], acc_s[h], q_ref[h], kv_ref[0, :, cols_h], kv_ref[1, :, cols_h], ok
            )
            m_s[h] = m
            l_s[h] = l
            acc_s[h] = acc

    full = start + block <= n_valid
    part = jnp.logical_and(start < n_valid, jnp.logical_not(full))
    pl.when(full)(lambda: body(False))
    pl.when(part)(lambda: body(True))

    @pl.when(j == pl.num_programs(0) - 1)
    def _():
        m_out[...] = m_s[...]
        l_out[...] = l_s[...]
        acc_out[...] = acc_s[...]


def own_attend(q, kv, n_valid):
    kv_heads, rows, _ = q.shape
    cache_len = kv.shape[1]
    block = min(OWN_BLOCK, cache_len)
    n_blocks = cache_len // block

    def kv_map(j, nv):
        last = jnp.maximum((nv[0] + block - 1) // block - 1, 0)
        return (0, jnp.minimum(j, last), 0)

    state_shapes = (
        jax.ShapeDtypeStruct((kv_heads, rows, 1), jnp.float32),
        jax.ShapeDtypeStruct((kv_heads, rows, 1), jnp.float32),
        jax.ShapeDtypeStruct((kv_heads, rows, HD), jnp.float32),
    )
    full3 = lambda j, nv: (0, 0, 0)
    return pl.pallas_call(
        functools.partial(own_kernel, kv_heads, block),
        out_shape=state_shapes,
        grid_spec=pltpu.PrefetchScalarGridSpec(
            num_scalar_prefetch=1,
            grid=(n_blocks,),
            in_specs=[
                pl.BlockSpec(q.shape, full3),
                pl.BlockSpec((2, block, kv.shape[2]), kv_map),
            ],
            out_specs=[pl.BlockSpec(s.shape, full3) for s in state_shapes],
            scratch_shapes=[pltpu.VMEM(s.shape, jnp.float32) for s in state_shapes],
        ),
        compiler_params=pltpu.CompilerParams(dimension_semantics=("arbitrary",)),
        cost_estimate=pl.CostEstimate(
            flops=4 * kv_heads * rows * cache_len * HD,
            transcendentals=kv_heads * rows * cache_len,
            bytes_accessed=kv.size * 2 + q.size * 2,
        ),
    )(n_valid, q, kv)


def shared_kernel(kv_heads, n_blocks, flag_ref, q_ref, m_ref, l_ref, acc_ref, *rest):
    blocks = rest[:n_blocks]
    dkv_ref, reach_ref = rest[n_blocks], rest[n_blocks + 1]
    m_out, l_out, acc_out = rest[n_blocks + 2:n_blocks + 5]
    for h in range(kv_heads):
        cols_h = slice(h * HD, (h + 1) * HD)
        q = q_ref[h]
        m, l, acc = m_ref[h], l_ref[h], acc_ref[h]
        for blk in blocks:
            m, l, acc = step(m, l, acc, q, blk[0, :, cols_h], blk[1, :, cols_h], None)
        m_out[h] = m
        l_out[h] = l
        acc_out[h] = acc

    @pl.when(flag_ref[0] == 1)
    def _():
        ok = reach_ref[...] > 0.5
        for h in range(kv_heads):
            cols_h = slice(h * HD, (h + 1) * HD)
            m, l, acc = step(
                m_out[h], l_out[h], acc_out[h], q_ref[h],
                dkv_ref[0, :, cols_h], dkv_ref[1, :, cols_h], ok,
            )
            m_out[h] = m
            l_out[h] = l
            acc_out[h] = acc


def shared_attend(q, state, blocks, draft_kv, reach_rows, flag):
    kv_heads, rows, _ = q.shape
    n_blocks = len(blocks)
    whole = lambda a: pl.BlockSpec(a.shape, lambda i, f: (0,) * a.ndim)
    operands = (q,) + tuple(state) + tuple(blocks) + (draft_kv, reach_rows)
    keys = sum(b.shape[1] for b in blocks)
    return pl.pallas_call(
        functools.partial(shared_kernel, kv_heads, n_blocks),
        out_shape=tuple(jax.ShapeDtypeStruct(s.shape, s.dtype) for s in state),
        grid_spec=pltpu.PrefetchScalarGridSpec(
            num_scalar_prefetch=1,
            grid=(1,),
            in_specs=[whole(a) for a in operands],
            out_specs=[whole(s) for s in state],
        ),
        compiler_params=pltpu.CompilerParams(vmem_limit_bytes=48 * 1024 * 1024),
        cost_estimate=pl.CostEstimate(
            flops=4 * kv_heads * rows * keys * HD,
            transcendentals=kv_heads * rows * keys,
            bytes_accessed=sum(b.size * 2 for b in blocks) + q.size * 2,
        ),
    )(flag, *operands)


def tree_reach(parent_row):
    node_count = parent_row.shape[0]
    nodes = jnp.arange(node_count, dtype=jnp.int32)
    reach = jnp.eye(node_count, dtype=jnp.float32) + (parent_row[:, None] == nodes[None, :]).astype(
        jnp.float32
    )
    for level_step in range(max(node_count - 1, 1).bit_length()):
        reach = jnp.minimum(jnp.dot(reach, reach, precision=lax.Precision.HIGHEST), 1.0)
    return reach > 0.5


def exchange_shared(shared_cache, group_ids, req_index, req_count):
    local = shared_cache[:, group_ids[req_index]]
    received = [local]
    pow2 = req_count & (req_count - 1) == 0
    for k in range(1, req_count):
        if pow2:
            pairs = [(r, r ^ k) for r in range(req_count)]
            dst = req_index ^ k
        else:
            pairs = [(r, (r + k) % req_count) for r in range(req_count)]
            dst = (req_index + k) % req_count
        sent = lax.dynamic_index_in_dim(shared_cache, group_ids[dst], 1, keepdims=False)
        received.append(lax.ppermute(sent, "req", pairs))
    return received


def shards(
    draft_query,
    draft_kv,
    own_cache,
    shared_cache,
    out_weight,
    lengths,
    group_ids,
    parents,
    accepted,
):
    kv_heads = own_cache.shape[3] // HD
    draft_len = draft_query.shape[1]
    rows = QPK * draft_len
    seq_count = lax.axis_size("seq")
    seq_index = lax.axis_index("seq")
    req_index = lax.axis_index("req")
    req_count = lax.axis_size("req")
    cache_len = own_cache.shape[2]

    blocks = exchange_shared(shared_cache, group_ids, req_index, req_count)

    queries = (
        draft_query[0]
        .reshape(draft_len, kv_heads, QPK, HD)
        .transpose(1, 2, 0, 3)
        .reshape(kv_heads, rows, HD)
    )
    n_valid = jnp.clip(lengths[0] - seq_index * cache_len, 0, cache_len).astype(jnp.int32)
    state = own_attend(queries, own_cache[0], n_valid.reshape(1))

    reach = tree_reach(parents[0])
    reach_rows = jnp.tile(reach.astype(jnp.float32), (QPK, 1))
    flag = (seq_index == 0).astype(jnp.int32).reshape(1)
    m, l, acc = shared_attend(queries, state, blocks, draft_kv[0], reach_rows, flag)

    heads_dev = kv_heads * QPK
    share = heads_dev // seq_count
    stats = jnp.stack([m.reshape(heads_dev, draft_len), l.reshape(heads_dev, draft_len)], 0)
    stats = lax.all_to_all(stats, "seq", 1, 1, tiled=True).reshape(2, seq_count, share, draft_len)
    acc = lax.all_to_all(acc.reshape(heads_dev, draft_len, HD), "seq", 0, 0, tiled=True)
    acc = acc.reshape(seq_count, share, draft_len, HD)
    part_max, part_total = stats[0], stats[1]
    final_max = jnp.max(part_max, axis=0)
    factor = jnp.exp(part_max - final_max[None])
    final_total = jnp.sum(part_total * factor, axis=0)
    final_sum = jnp.sum(acc * factor[..., None], axis=0)
    attended = (final_sum / final_total[..., None]).astype(jnp.bfloat16)
    attended = jnp.transpose(attended, (1, 0, 2)).reshape(draft_len, share * HD)
    out_piece = lax.psum_scatter(
        lax.dot_general(
            out_weight, attended, (((0,), (1,)), ((), ())), preferred_element_type=jnp.float32
        ),
        ("tensor", "seq"),
        scatter_dimension=0,
        tiled=True,
    )
    verified = out_piece.T[None].astype(jnp.bfloat16)
    accepted_kv = jnp.take(draft_kv[0], accepted[0], axis=1)[None]
    return (verified, accepted_kv)


def solution(mesh):
    placed = (
        P("req", None, "tensor"),
        P("req", None, None, "tensor"),
        P("req", None, "seq", "tensor"),
        P(None, None, ("req", "seq"), "tensor"),
        P(("tensor", "seq"), None),
        P("req"),
        P(),
        P("req", None),
        P("req", None),
    )
    return jax.shard_map(
        shards,
        mesh=mesh,
        in_specs=placed,
        out_specs=(P("req", None, ("tensor", "seq")), P("req", None, None, "tensor")),
        check_vma=False,
    )
```

time: 320 us -> 227 us (0.71)
  Pallas kernels: 0 us -> 104 us
  matrix products: 112 us -> 12 us
  local copies, waits for them, and re-layouts: 62.2 us -> 12.4 us
  other arithmetic: 52.8 us -> 3.48 us
  starting transfers between devices: 0.12 us -> 7.05 us
  between operations: 16 us -> 22.5 us
  blocking collectives: 10.9 us -> 6.21 us
  waiting for transfers between devices: 61.1 us -> 57.4 us
    pallas_call x0 -> x2, Pallas kernels: none -> 104 us  [the longest x1 80 us: own_attend(): pl.pallas_call(functools.partial(own_kernel, kv_heads, block), out_shape=...]
    dot_general x12 -> x0, matrix products: 100 us -> none  [the longest x5 55.8 us: update(): jnp.einsum('hrk,khd->hrd', weights.astype(jnp.bfloat16), value_block, pre...]
    reduce_sum x6 -> x2, other arithmetic: 41.7 us -> 0.35 us  [the longest x1 0.34 us: shards(): final_sum = jnp.sum(acc * factor[..., None], axis=0)]
    while x12 -> x0, local copies, waits for them, and re-layouts: 25.5 us -> none
    slice x9 -> x1, local copies, waits for them, and re-layouts: 22.4 us -> 0.03 us  [shards(): part_max, part_total = (stats[0], stats[1])]
    all_gather x2 -> x0, waiting for transfers between devices: 21.3 us -> none  [the longest x1 21.3 us: merged(): pieces = jax.tree.map(lambda part: lax.all_gather(part, axis), value)]
    all_to_all x0 -> x1, waiting for transfers between devices: none -> 13 us  [shards(): lax.all_to_all(acc.reshape(heads_dev, draft_len, HD), 'seq', 0, 0, tiled=...]
    all_gather x2 -> x0, blocking collectives: 10.9 us -> none  [merged(): pieces = jax.tree.map(lambda part: lax.all_gather(part, axis), value)]
  transfers between devices with their start and end apart: 3 -> 5, of which waited for: 2 -> 3; matrix products, arithmetic and copies ran while one was open for 53% -> 3% of each run, Pallas kernels for 0% -> 36%
where the time goes in v1:
time: 227 us; the launch traced here: 225 us
  Pallas kernels  104 us (46%)
  waiting for transfers between devices  57.4 us (25%)
  between operations  22.5 us (10%)
  local copies, waits for them, and re-layouts  12.4 us (5%)
  matrix products  12 us (5%)
  starting transfers between devices  7.05 us (3%)
  blocking collectives  6.21 us (3%)
  other arithmetic  3.48 us (2%)
    pallas_call x1, Pallas kernels, own_attend(): pl.pallas_call(functools.partial(own_kernel, kv_heads, block), out_shape=...  80 us
    reduce_scatter x1, waiting for transfers between devices, shards(): lax.psum_scatter(lax.dot_general(out_weight, attended, (((0,), (1,)), (()...  39 us
    pallas_call x1, Pallas kernels, shared_attend(): pl.pallas_call(functools.partial(shared_kernel, kv_heads, n_blocks), out_...  24.1 us
    all_to_all x1, waiting for transfers between devices, shards(): lax.all_to_all(acc.reshape(heads_dev, draft_len, HD), 'seq', 0, 0, tiled=...  13 us
    dot_general x1, matrix products, shards(): lax.dot_general(out_weight, attended, (((0,), (1,)), ((), ())), preferred...  10.2 us
    all_to_all x1, blocking collectives, shards(): lax.all_to_all(stats, 'seq', 1, 1, tiled=True)  6.21 us
    ppermute x3, waiting for transfers between devices, exchange_shared(): received.append(lax.ppermute(sent, 'req', pairs))  5.42 us
  transfers between devices with their start and end apart: 5, of which 3 were waited for; matrix products, arithmetic and copies ran while one was open for 3% of the time, Pallas kernels for 36%

profile of v1, /device:TPU:8, one launch (start us, length us, event | category | flops | bytes accessed | tf_op | source)
XLA Modules:
  0.0 225.2 jit_solution(9711715119510736544)
XLA Ops:
  7.2 1.5 fusion.12
  16.3 3.9 %dynamic-slice_bitcast_fusion = (bf16[2,512,512]{2,1,0:T(8,128)(2,1)S(1)}, bf16[2,512,512]{2,1,0:T(8,128)(2,1)}, bf16[2,512,512]{2,1,0:T(8,128)(2,1)}, bf16[2,512,512]{2,1,0:T(8,128)(2,1)S(1)}) fusion(bf16[2,2,512,512]{3,2,1,0:T(8,128)(2,1)} %param.12, s32[]{:T(128)S(6)} %select_n.59, s32[]{:T(128)S(6)} %select_n.55, s32[]{:T(128)S(6)} %select_n.53, ...), kind=kLoop, calls=%fused_computation.11 | loop fusion | bytes 8388624 | tf_op jit(solution)/shard_map/jit(dynamic_index_in_dim)/squeeze | solution.py:185
  20.2 0.0 collective-permute-start
  20.2 3.0 %collective-permute-start.1 = (bf16[2,512,512]{2,1,0:T(8,128)(2,1)S(1)}, bf16[2,512,512]{2,1,0:T(8,128)(2,1)}, u32[]{:S(2)}, u32[]{:S(2)}) collective-permute-start(bf16[2,512,512]{2,1,0:T(8,128)(2,1)S(1)} %get-tuple-element.23), channel_id=1, source_target_pairs={{0,8},{4,12},{8,0},{12,4},{1,9},{5,13},{9,1},{13,5},{2,10},{6,14},... | collective-permute-start | bytes 3145736 | tf_op jit(solution)/shard_map/ppermute | solution.py:186
  23.3 0.5 collective-permute-start.2
  23.7 1.0 convolution_minimum_fusion.5
  24.7 0.2 convolution_minimum_fusion.4
  24.9 0.2 convolution_minimum_fusion.3
  25.0 0.2 convolution_minimum_fusion.2
  25.2 0.2 convolution_minimum_fusion.1
  26.0 1.1 copy.21
  27.2 0.0 copy-start.3
  27.2 1.1 copy.15
  28.3 0.0 copy-start
  28.3 0.2 fusion.1
  28.4 80.0 %shard_map.104 = (f32[4,512,1]{2,1,0:T(8,128)}, f32[4,512,1]{2,1,0:T(8,128)}, f32[4,512,128]{2,1,0:T(8,128)}) custom-call(s32[1]{0:T(128)} %bitcast.4.nv_ref, bf16[4,512,128]{2,1,0:T(8,128)(2,1)} %bitcast.78, bf16[2,8192,512]{2,1,0:T(8,128)(2,1)} %bitcast.92), custom_call_target="tpu_custom_call" | custom-call | flops 8589934592 | bytes 17301504 | tf_op jit(solution)/shard_map/pallas_call | solution.py:89
  108.5 0.0 collective-permute-done.rest_1_
  108.5 0.0 collective-permute-done.1.rest_2_
  108.5 5.4 %collective-permute-done.2.rest_3_ = bf16[2,512,512]{2,1,0:T(8,128)(2,1)} collective-permute-done((bf16[2,512,512]{2,1,0:T(8,128)(2,1)S(1)}, bf16[2,512,512]{2,1,0:T(8,128)(2,1)}, u32[]{:S(2)}, u32[]{:S(2)}) %collective-permute-start.2) | collective-permute-done | bytes 1048608 | tf_op jit(solution)/shard_map/ppermute | solution.py:186
  113.9 0.0 copy-done.3
  113.9 0.0 copy-done
  113.9 0.0 copy-start.1
  113.9 1.2 copy-done.1
  115.2 0.0 copy-start.2
  115.2 1.2 copy-done.2
  116.4 24.1 %shard_map.105 = (f32[4,512,1]{2,1,0:T(8,128)S(1)}, f32[4,512,1]{2,1,0:T(8,128)S(1)}, f32[4,512,128]{2,1,0:T(8,128)}) custom-call(s32[1]{0:T(128)} %bitcast.flag_ref, bf16[4,512,128]{2,1,0:T(8,128)(2,1)S(1)} %bitcast.79, f32[4,512,1]{2,1,0:T(8,128)S(1)} %copy-done.1, f32[4,512,1]{2,1,0:T(8,128)S(1)} %copy-done.2, f32[4,512,128]{2,1,0:T(8,128)} %get-tuple-element.10.acc_ref, ...), custom_call_target="tpu_custom_call" | custom-call | flops 2147483648 | bytes 4718592 | tf_op jit(solution)/shard_map/pallas_call | solution.py:145
  140.5 0.0 copy-start.4
  140.5 0.3 reduce
  140.9 0.1 stack_reshape.6
  140.9 0.4 reduce.1
  141.3 0.1 stack_reshape.7
  141.4 0.1 reshape.107
  141.5 6.2 %all_to_all.10 = f32[4,1,1024]{2,1,0:T(1,128)S(1)} all-to-all(f32[4,1,1024]{2,1,0:T(1,128)S(1)} %reshape.107), channel_id=1, replica_groups=mesh['tensor'=2,'req'=4,'seq'=4] {'seq'}, dimensions={0} | all-to-all | bytes 32768 | tf_op jit(solution)/shard_map/all_to_all | solution.py:229
  147.7 3.5 %all-to-all-start = ((f32[32,64,128]{2,1,0:T(8,128)}), f32[32,64,128]{2,1,0:T(8,128)S(1)}, u32[]{:S(2)}, u32[]{:S(2)}) async-start(f32[32,64,128]{2,1,0:T(8,128)} %bitcast.18), calls=%async_computation | async-start | bytes 2097152 | tf_op jit(solution)/shard_map/all_to_all | solution.py:230
  151.3 0.0 reduce-scatter.2.cloned.1.call-start
  151.3 0.5 broadcast.79
  151.8 0.7 reduce.2
  152.5 0.1 reshape.108
  152.7 13.0 %all-to-all-done = f32[32,64,128]{2,1,0:T(8,128)S(1)} async-done(((f32[32,64,128]{2,1,0:T(8,128)}), f32[32,64,128]{2,1,0:T(8,128)S(1)}, u32[]{:S(2)}, u32[]{:S(2)}) %all-to-all-start) | async-done | bytes 1048608 | tf_op jit(solution)/shard_map/all_to_all | solution.py:230
  165.7 0.3 multiply_reduce_fusion
  166.0 10.2 %convolution_bitcast_fusion = f32[8192,64]{0,1:T(8,128)} fusion(bf16[1024,8192]{1,0:T(8,128)(2,1)} %param.13, f32[64,8]{0,1:T(8,128)S(1)} %bitcast.90, f32[8,64,128]{2,1,0:T(8,128)S(1)} %multiply_reduce_fusion), kind=kOutput, calls=%fused_computation.1 | convolution fusion | flops 1073872896 | bytes 19138560 | tf_op jit(solution)/shard_map/dot_general | solution.py:240
  176.2 0.0 reduce-scatter.2.cloned.1.call-update
  176.3 0.1 copy.18
  176.4 0.0 copy-done.4
  176.4 0.6 gather_fusion
  177.0 0.1 broadcast_select_fusion
  177.1 0.6 copy.19
  177.7 39.0 %reduce-scatter.2.cloned.1.call-done = f32[1024,64]{0,1:T(8,128)} async-done(((f32[8192,64]{0,1:T(8,128)}), f32[1024,64]{0,1:T(8,128)}) %reduce-scatter.2.cloned.1.call-update) | async-done | bytes 262160 | tf_op jit(solution)/shard_map/reduce_scatter | solution.py:239
  216.7 1.6 convert_bitcast_fusion
  (9 shorter events, 0.1 us)
Async XLA Ops:
  20.2 88.2 %collective-permute-start = (bf16[2,512,512]{2,1,0:T(8,128)(2,1)}, bf16[2,512,512]{2,1,0:T(8,128)(2,1)}, u32[]{:S(2)}, u32[]{:S(2)}) collective-permute-start(bf16[2,512,512]{2,1,0:T(8,128)(2,1)} %get-tuple-element.21), channel_id=1, source_target_pairs={{0,4},{4,0},{8,12},{12,8},{1,5},{5,1},{9,13},{13,9},{2,6},{6,2},{1... | collective-permute-start | bytes 3145736 | tf_op jit(solution)/shard_map/ppermute | solution.py:186
  20.2 88.2 %collective-permute-start.1 = (bf16[2,512,512]{2,1,0:T(8,128)(2,1)S(1)}, bf16[2,512,512]{2,1,0:T(8,128)(2,1)}, u32[]{:S(2)}, u32[]{:S(2)}) collective-permute-start(bf16[2,512,512]{2,1,0:T(8,128)(2,1)S(1)} %get-tuple-element.23), channel_id=1, source_target_pairs={{0,8},{4,12},{8,0},{12,4},{1,9},{5,13},{9,1},{13,5},{2,10},{6,14},... | collective-permute-start | bytes 3145736 | tf_op jit(solution)/shard_map/ppermute | solution.py:186
  23.3 90.6 %collective-permute-start.2 = (bf16[2,512,512]{2,1,0:T(8,128)(2,1)S(1)}, bf16[2,512,512]{2,1,0:T(8,128)(2,1)}, u32[]{:S(2)}, u32[]{:S(2)}) collective-permute-start(bf16[2,512,512]{2,1,0:T(8,128)(2,1)S(1)} %get-tuple-element.20), channel_id=1, source_target_pairs={{0,12},{4,8},{8,4},{12,0},{1,13},{5,9},{9,5},{13,1},{2,14},{6,10},... | collective-permute-start | bytes 3145736 | tf_op jit(solution)/shard_map/ppermute | solution.py:186
  27.2 86.7 %copy-start.3 = (bf16[1,2,64,512]{3,2,1,0:T(8,128)(2,1)S(1)}, bf16[1,2,64,512]{3,2,1,0:T(8,128)(2,1)}, u32[]{:S(2)}) copy-start(bf16[1,2,64,512]{3,2,1,0:T(8,128)(2,1)} %param.10) | copy-start | bytes 393220
  28.3 85.7 %copy-start = (bf16[64,4,8,128]{3,0,2,1:T(8,128)(2,1)S(1)}, bf16[64,4,8,128]{3,0,2,1:T(8,128)(2,1)}, u32[]{:S(2)}) copy-start(bf16[64,4,8,128]{3,0,2,1:T(8,128)(2,1)} %copy.15) | copy-start | bytes 1572868
  113.9 1.2 copy-start.1
  115.2 1.2 copy-start.2
  140.5 35.9 %copy-start.4 = (s32[1,8]{1,0:T(1,128)S(1)}, s32[1,8]{1,0:T(1,128)}, u32[]{:S(2)}) copy-start(s32[1,8]{1,0:T(1,128)} %param.17) | copy-start | bytes 100
  147.7 17.9 %all-to-all-start = ((f32[32,64,128]{2,1,0:T(8,128)}), f32[32,64,128]{2,1,0:T(8,128)S(1)}, u32[]{:S(2)}, u32[]{:S(2)}) async-start(f32[32,64,128]{2,1,0:T(8,128)} %bitcast.18), calls=%async_computation | async-start | bytes 2097152 | tf_op jit(solution)/shard_map/all_to_all | solution.py:230
  151.3 65.5 %reduce-scatter.2.cloned.1.call-start = ((), (), s32[]{:S(2)}) async-start(), calls=%async_computation.3 | async-start | bytes 2359296 | tf_op jit(solution)/shard_map/reduce_scatter | solution.py:239
Sparse Core Ops, SparseCore 0:
  176.4 40.3 reduce-scatter.1

commit v2 on v1

--- a/solution.py
+++ b/solution.py
@@ -11,28 +11,28 @@
 QPK = 8
 NEG_FILL = -1e30
 SCALE = HD ** (-0.5)
+EXP2_SCALE = SCALE * 1.4426950408889634
 OWN_BLOCK = 512
 
 
-def step(m_prev, l_prev, acc_prev, q, k, v, ok):
+def step(m_prev, l_prev, acc_prev, q, k, v, ones, ok):
     scores = lax.dot_general(
         q, k, (((1,), (1,)), ((), ())), preferred_element_type=jnp.float32
-    ) * SCALE
+    )
     if ok is not None:
         scores = jnp.where(ok, scores, NEG_FILL)
     m_new = jnp.maximum(m_prev, jnp.max(scores, axis=1, keepdims=True))
-    alpha = jnp.exp(m_prev - m_new)
-    weights = jnp.exp(scores - m_new)
+    alpha = jnp.exp2((m_prev - m_new) * EXP2_SCALE)
+    weights = jnp.exp2((scores - m_new) * EXP2_SCALE)
     if ok is not None:
         weights = jnp.where(ok, weights, 0.0)
-    l_new = alpha * l_prev + jnp.sum(weights, axis=1, keepdims=True)
-    acc_new = alpha * acc_prev + jnp.dot(
-        weights.astype(jnp.bfloat16), v, preferred_element_type=jnp.float32
-    )
+    weights = weights.astype(jnp.bfloat16)
+    l_new = alpha * l_prev + jnp.dot(weights, ones, preferred_element_type=jnp.float32)
+    acc_new = alpha * acc_prev + jnp.dot(weights, v, preferred_element_type=jnp.float32)
     return m_new, l_new, acc_new
 
 
-def own_kernel(kv_heads, block, nv_ref, q_ref, kv_ref, m_out, l_out, acc_out, m_s, l_s, acc_s):
+def own_kernel(kv_heads, block, nv_ref, q_ref, kv_ref, ones_ref, m_out, l_out, acc_out, m_s, l_s, acc_s):
     j = pl.program_id(0)
     n_valid = nv_ref[0]
 
@@ -52,7 +52,8 @@
         for h in range(kv_heads):
             cols_h = slice(h * HD, (h + 1) * HD)
             m, l, acc = step(
-                m_s[h], l_s[h], acc_s[h], q_ref[h], kv_ref[0, :, cols_h], kv_ref[1, :, cols_h], ok
+                m_s[h], l_s[h], acc_s[h], q_ref[h], kv_ref[0, :, cols_h], kv_ref[1, :, cols_h],
+                ones_ref[...], ok,
             )
             m_s[h] = m
             l_s[h] = l
@@ -82,9 +83,10 @@
 
     state_shapes = (
         jax.ShapeDtypeStruct((kv_heads, rows, 1), jnp.float32),
-        jax.ShapeDtypeStruct((kv_heads, rows, 1), jnp.float32),
         jax.ShapeDtypeStruct((kv_heads, rows, HD), jnp.float32),
-    )
+        jax.ShapeDtypeStruct((kv_heads, rows, HD), jnp.float32),
+    )
+    ones = jnp.ones((block, HD), jnp.bfloat16)
     full3 = lambda j, nv: (0, 0, 0)
     return pl.pallas_call(
         functools.partial(own_kernel, kv_heads, block),
@@ -95,29 +97,32 @@
             in_specs=[
                 pl.BlockSpec(q.shape, full3),
                 pl.BlockSpec((2, block, kv.shape[2]), kv_map),
+                pl.BlockSpec(ones.shape, lambda j, nv: (0, 0)),
             ],
             out_specs=[pl.BlockSpec(s.shape, full3) for s in state_shapes],
             scratch_shapes=[pltpu.VMEM(s.shape, jnp.float32) for s in state_shapes],
         ),
         compiler_params=pltpu.CompilerParams(dimension_semantics=("arbitrary",)),
         cost_estimate=pl.CostEstimate(
-            flops=4 * kv_heads * rows * cache_len * HD,
+            flops=6 * kv_heads * rows * cache_len * HD,
             transcendentals=kv_heads * rows * cache_len,
             bytes_accessed=kv.size * 2 + q.size * 2,
         ),
-    )(n_valid, q, kv)
+    )(n_valid, q, kv, ones)
 
 
 def shared_kernel(kv_heads, n_blocks, flag_ref, q_ref, m_ref, l_ref, acc_ref, *rest):
     blocks = rest[:n_blocks]
-    dkv_ref, reach_ref = rest[n_blocks], rest[n_blocks + 1]
-    m_out, l_out, acc_out = rest[n_blocks + 2:n_blocks + 5]
+    dkv_ref, reach_ref, ones_ref, tree_ones_ref = rest[n_blocks:n_blocks + 4]
+    m_out, l_out, acc_out = rest[n_blocks + 4:n_blocks + 7]
     for h in range(kv_heads):
         cols_h = slice(h * HD, (h + 1) * HD)
         q = q_ref[h]
         m, l, acc = m_ref[h], l_ref[h], acc_ref[h]
         for blk in blocks:
-            m, l, acc = step(m, l, acc, q, blk[0, :, cols_h], blk[1, :, cols_h], None)
+            m, l, acc = step(
+                m, l, acc, q, blk[0, :, cols_h], blk[1, :, cols_h], ones_ref[...], None
+            )
         m_out[h] = m
         l_out[h] = l
         acc_out[h] = acc
@@ -129,7 +134,7 @@
             cols_h = slice(h * HD, (h + 1) * HD)
             m, l, acc = step(
                 m_out[h], l_out[h], acc_out[h], q_ref[h],
-                dkv_ref[0, :, cols_h], dkv_ref[1, :, cols_h], ok,
+                dkv_ref[0, :, cols_h], dkv_ref[1, :, cols_h], tree_ones_ref[...], ok,
             )
             m_out[h] = m
             l_out[h] = l
@@ -140,7 +145,9 @@
     kv_heads, rows, _ = q.shape
     n_blocks = len(blocks)
     whole = lambda a: pl.BlockSpec(a.shape, lambda i, f: (0,) * a.ndim)
-    operands = (q,) + tuple(state) + tuple(blocks) + (draft_kv, reach_rows)
+    ones = jnp.ones((blocks[0].shape[1], HD), jnp.bfloat16)
+    tree_ones = jnp.ones((draft_kv.shape[1], HD), jnp.bfloat16)
+    operands = (q,) + tuple(state) + tuple(blocks) + (draft_kv, reach_rows, ones, tree_ones)
     keys = sum(b.shape[1] for b in blocks)
     return pl.pallas_call(
         functools.partial(shared_kernel, kv_heads, n_blocks),
@@ -153,7 +160,7 @@
         ),
         compiler_params=pltpu.CompilerParams(vmem_limit_bytes=48 * 1024 * 1024),
         cost_estimate=pl.CostEstimate(
-            flops=4 * kv_heads * rows * keys * HD,
+            flops=6 * kv_heads * rows * keys * HD,
             transcendentals=kv_heads * rows * keys,
             bytes_accessed=sum(b.size * 2 for b in blocks) + q.size * 2,
         ),
@@ -225,26 +232,32 @@
 
     heads_dev = kv_heads * QPK
     share = heads_dev // seq_count
-    stats = jnp.stack([m.reshape(heads_dev, draft_len), l.reshape(heads_dev, draft_len)], 0)
-    stats = lax.all_to_all(stats, "seq", 1, 1, tiled=True).reshape(2, seq_count, share, draft_len)
-    acc = lax.all_to_all(acc.reshape(heads_dev, draft_len, HD), "seq", 0, 0, tiled=True)
-    acc = acc.reshape(seq_count, share, draft_len, HD)
-    part_max, part_total = stats[0], stats[1]
+    stats = jnp.concatenate(
+        [m[..., 0].reshape(heads_dev, draft_len), l[..., 0].reshape(heads_dev, draft_len)], 1
+    )
+    packed = jnp.concatenate(
+        [acc.reshape(heads_dev, draft_len, HD), stats.reshape(heads_dev, 1, 2 * draft_len)], 1
+    )
+    packed = lax.all_to_all(packed, "seq", 0, 0, tiled=True)
+    packed = packed.reshape(seq_count, share, draft_len + 1, 2 * draft_len)
+    part_max = packed[:, :, draft_len, :draft_len]
+    part_total = packed[:, :, draft_len, draft_len:]
+    part_sum = packed[:, :, :draft_len, :]
     final_max = jnp.max(part_max, axis=0)
-    factor = jnp.exp(part_max - final_max[None])
+    factor = jnp.exp2((part_max - final_max[None]) * EXP2_SCALE)
     final_total = jnp.sum(part_total * factor, axis=0)
-    final_sum = jnp.sum(acc * factor[..., None], axis=0)
+    final_sum = jnp.sum(part_sum * factor[..., None], axis=0)
     attended = (final_sum / final_total[..., None]).astype(jnp.bfloat16)
     attended = jnp.transpose(attended, (1, 0, 2)).reshape(draft_len, share * HD)
     out_piece = lax.psum_scatter(
         lax.dot_general(
             out_weight, attended, (((0,), (1,)), ((), ())), preferred_element_type=jnp.float32
-        ),
+        ).astype(jnp.bfloat16),
         ("tensor", "seq"),
         scatter_dimension=0,
         tiled=True,
     )
-    verified = out_piece.T[None].astype(jnp.bfloat16)
+    verified = out_piece.T[None]
     accepted_kv = jnp.take(draft_kv[0], accepted[0], axis=1)[None]
     return (verified, accepted_kv)
 

time: 227 us -> 208 us (0.916)
  Pallas kernels: 104 us -> 74.8 us
  blocking collectives: 6.21 us -> 18.3 us
  waiting for transfers between devices: 57.4 us -> 61.5 us
  starting transfers between devices: 7.05 us -> 3.53 us
  other arithmetic: 3.48 us -> 1.06 us
    ppermute x3, waiting for transfers between devices: 5.42 us -> 28.1 us  [exchange_shared(): received.append(lax.ppermute(sent, 'req', pairs))]
    pallas_call x1, Pallas kernels: 80 us -> 57.5 us  [own_attend(): pl.pallas_call(functools.partial(own_kernel, kv_heads, block), out_shape=...]
    all_to_all x1 -> x0, waiting for transfers between devices: 13 us -> none  [shards(): lax.all_to_all(acc.reshape(heads_dev, draft_len, HD), 'seq', 0, 0, tiled=...]
    all_to_all x1, blocking collectives: 6.21 us -> 18.3 us  [shards(): packed = lax.all_to_all(packed, 'seq', 0, 0, tiled=True)]
    pallas_call x1, Pallas kernels: 24.1 us -> 17.4 us  [shared_attend(): pl.pallas_call(functools.partial(shared_kernel, kv_heads, n_blocks), out_...]
    reduce_scatter x1, waiting for transfers between devices: 39 us -> 33.4 us  [shards(): lax.psum_scatter(lax.dot_general(out_weight, attended, (((0,), (1,)), (()...]
    all_to_all x1 -> x0, starting transfers between devices: 3.52 us -> none  [shards(): lax.all_to_all(acc.reshape(heads_dev, draft_len, HD), 'seq', 0, 0, tiled=...]
  transfers between devices with their start and end apart: 5 -> 4, of which waited for: 3 -> 3; matrix products, arithmetic and copies ran while one was open for 3% -> 3% of each run, Pallas kernels for 36% -> 28%
where the time goes in v2:
time: 208 us; the launch traced here: 205 us
  Pallas kernels  74.8 us (36%)
  waiting for transfers between devices  61.5 us (30%)
  between operations  22.5 us (11%)
  blocking collectives  18.3 us (9%)
  local copies, waits for them, and re-layouts  12.8 us (6%)
  matrix products  10.9 us (5%)
  starting transfers between devices  3.53 us (2%)
    pallas_call x1, Pallas kernels, own_attend(): pl.pallas_call(functools.partial(own_kernel, kv_heads, block), out_shape=...  57.5 us
    reduce_scatter x1, waiting for transfers between devices, shards(): lax.psum_scatter(lax.dot_general(out_weight, attended, (((0,), (1,)), (()...  33.4 us
    ppermute x3, waiting for transfers between devices, exchange_shared(): received.append(lax.ppermute(sent, 'req', pairs))  28.1 us
    all_to_all x1, blocking collectives, shards(): packed = lax.all_to_all(packed, 'seq', 0, 0, tiled=True)  18.3 us
    pallas_call x1, Pallas kernels, shared_attend(): pl.pallas_call(functools.partial(shared_kernel, kv_heads, n_blocks), out_...  17.4 us
    dot_general x1, matrix products, shards(): lax.dot_general(out_weight, attended, (((0,), (1,)), ((), ())), preferred...  9.86 us
    unnamed x14, local copies, waits for them, and re-layouts  4.5 us
  transfers between devices with their start and end apart: 4, of which 3 were waited for; matrix products, arithmetic and copies ran while one was open for 3% of the time, Pallas kernels for 28%

profile of v2, /device:TPU:8, one launch (start us, length us, event | category | flops | bytes accessed | tf_op | source)
XLA Modules:
  0.0 205.5 jit_solution(14032488460167514578)
XLA Ops:
  7.2 0.0 reduce-scatter.2.cloned.1.call-start
  7.2 1.5 fusion.19
  16.3 3.6 %dynamic-slice_bitcast_fusion = (bf16[2,512,512]{2,1,0:T(8,128)(2,1)S(1)}, bf16[2,512,512]{2,1,0:T(8,128)(2,1)S(1)}, bf16[2,512,512]{2,1,0:T(8,128)(2,1)}, bf16[2,512,512]{2,1,0:T(8,128)(2,1)S(1)}) fusion(bf16[2,2,512,512]{3,2,1,0:T(8,128)(2,1)} %param.12, s32[]{:T(128)S(6)} %select_n.59, s32[]{:T(128)S(6)} %select_n.55, s32[]{:T(128)S(6)} %select_n.53, ...), kind=kLoop, calls=%fused_computation.16 | loop fusion | bytes 8388624 | tf_op jit(solution)/shard_map/jit(dynamic_index_in_dim)/squeeze | solution.py:192
  20.0 0.0 copy-start.4
  20.0 0.0 collective-permute-start
  20.0 3.1 %collective-permute-start.1 = (bf16[2,512,512]{2,1,0:T(8,128)(2,1)S(1)}, bf16[2,512,512]{2,1,0:T(8,128)(2,1)}, u32[]{:S(2)}, u32[]{:S(2)}) collective-permute-start(bf16[2,512,512]{2,1,0:T(8,128)(2,1)S(1)} %get-tuple-element.23), channel_id=1, source_target_pairs={{0,8},{4,12},{8,0},{12,4},{1,9},{5,13},{9,1},{13,5},{2,10},{6,14},... | collective-permute-start | bytes 3145736 | tf_op jit(solution)/shard_map/ppermute | solution.py:193
  23.0 0.4 collective-permute-start.2
  24.1 1.1 copy.28
  25.3 1.0 copy.18
  26.2 0.0 copy-done.4
  26.2 0.2 convolution_minimum_fusion.5
  26.5 0.2 convolution_minimum_fusion.4
  26.7 0.2 convolution_minimum_fusion.3
  26.8 0.2 convolution_minimum_fusion.2
  27.0 0.2 convolution_minimum_fusion.1
  27.2 0.2 fusion.2
  27.3 0.7 broadcast_11_ones_ref_rest_6_.2.ones_ref.rest_6_
  28.0 0.0 copy-start.1
  28.0 0.0 copy-start.2
  28.0 57.5 %shard_map.104 = (f32[4,512,1]{2,1,0:T(8,128)}, f32[4,512,128]{2,1,0:T(8,128)}, f32[4,512,128]{2,1,0:T(8,128)}) custom-call(s32[1]{0:T(128)} %bitcast.4.nv_ref, bf16[4,512,128]{2,1,0:T(8,128)(2,1)} %bitcast.92, bf16[2,8192,512]{2,1,0:T(8,128)(2,1)} %bitcast.104, bf16[512,128]{1,0:T(8,128)(2,1)} %broadcast_11_ones_ref_rest_6_.2.ones_ref.rest_6_), custom_call_target="tpu_custom_call" | custom-call | flops 12884901888 | bytes 17301504 | tf_op jit(solution)/shard_map/pallas_call | solution.py:91
  85.5 0.0 collective-permute-done.rest_1_
  85.5 6.0 %collective-permute-done.1.rest_2_ = bf16[2,512,512]{2,1,0:T(8,128)(2,1)} collective-permute-done((bf16[2,512,512]{2,1,0:T(8,128)(2,1)S(1)}, bf16[2,512,512]{2,1,0:T(8,128)(2,1)}, u32[]{:S(2)}, u32[]{:S(2)}) %collective-permute-start.1) | collective-permute-done | bytes 1048608 | tf_op jit(solution)/shard_map/ppermute | solution.py:193
  91.5 22.1 %collective-permute-done.2.rest_3_ = bf16[2,512,512]{2,1,0:T(8,128)(2,1)} collective-permute-done((bf16[2,512,512]{2,1,0:T(8,128)(2,1)S(1)}, bf16[2,512,512]{2,1,0:T(8,128)(2,1)}, u32[]{:S(2)}, u32[]{:S(2)}) %collective-permute-start.2) | collective-permute-done | bytes 1048608 | tf_op jit(solution)/shard_map/ppermute | solution.py:193
  113.6 0.0 copy-done.1
  113.6 0.0 copy-done.2
  113.7 0.0 copy-start
  113.7 1.0 copy-done
  114.7 0.0 copy-start.3
  114.7 1.2 copy-done.3
  115.9 17.4 %shard_map.105 = (f32[4,512,1]{2,1,0:T(8,128)S(1)}, f32[4,512,128]{2,1,0:T(8,128)S(1)}, f32[4,512,128]{2,1,0:T(8,128)S(1)}) custom-call(s32[1]{0:T(128)} %bitcast.flag_ref, bf16[4,512,128]{2,1,0:T(8,128)(2,1)S(1)} %bitcast.93, f32[4,512,1]{2,1,0:T(8,128)S(1)} %copy-done.3, f32[4,512,128]{2,1,0:T(8,128)} %get-tuple-element.9.l_ref, ...), custom_call_target="tpu_custom_call" | custom-call | flops 3221225472 | bytes 4718592 | tf_op jit(solution)/shard_map/pallas_call | solution.py:152
  133.3 0.3 reduce.1
  133.6 0.1 reshape_squeeze.10
  133.7 0.4 slice_reduce_fusion
  134.1 0.1 reshape_squeeze.11
  134.2 0.1 pad_maximum_fusion.1
  134.2 0.1 pad_maximum_fusion
  134.3 18.3 %all_to_all.5 = f32[32,65,128]{2,1,0:T(8,128)S(1)} all-to-all(f32[32,65,128]{2,1,0:T(8,128)S(1)} %pad_maximum_fusion), channel_id=1, replica_groups=mesh['tensor'=2,'req'=4,'seq'=4] {'seq'}, dimensions={0} | all-to-all | bytes 2129920 | tf_op jit(solution)/shard_map/all_to_all | solution.py:241
  152.6 0.2 copy.43
  152.8 0.1 fusion.13
  152.9 0.1 copy.21
  153.0 0.3 fusion.3
  153.4 9.9 %fusion = bf16[8192,64]{0,1:T(8,128)(2,1)} fusion(bf16[1024,8192]{1,0:T(8,128)(2,1)} %param.13, f32[64,8]{0,1:T(8,128)S(1)} %bitcast.102, f32[8,64,128]{2,0,1:T(8,128)S(1)} %fusion.3), kind=kOutput, calls=%fused_computation.2 | convolution fusion | flops 1074397184 | bytes 18089984 | tf_op jit(solution)/shard_map/dot_general | solution.py:253
  163.2 0.0 copy-start.5
  163.2 0.0 reduce-scatter.2.cloned.1.call-update
  163.3 0.1 copy.24
  163.4 0.5 copy-done.5
  163.9 0.6 gather_fusion
  164.5 0.1 broadcast_select_fusion
  164.6 0.6 copy.25
  165.2 33.4 %reduce-scatter.2.cloned.1.call-done = bf16[1024,64]{0,1:T(8,128)(2,1)} async-done(((bf16[8192,64]{0,1:T(8,128)(2,1)}), bf16[1024,64]{0,1:T(8,128)(2,1)}) %reduce-scatter.2.cloned.1.call-update) | async-done | bytes 131088 | tf_op jit(solution)/shard_map/reduce_scatter | solution.py:252
  (6 shorter events, 0.1 us)
Async XLA Ops:
  7.2 191.4 %reduce-scatter.2.cloned.1.call-start = ((), (), s32[]{:S(2)}) async-start(), calls=%async_computation.2 | async-start | bytes 1179648 | tf_op jit(solution)/shard_map/reduce_scatter | solution.py:252
  20.0 6.3 %copy-start.4 = (s32[1,64]{1,0:T(1,128)S(1)}, s32[1,64]{1,0:T(1,128)}, u32[]{:S(2)}) copy-start(s32[1,64]{1,0:T(1,128)} %param.16) | copy-start | bytes 772
  20.0 65.5 %collective-permute-start = (bf16[2,512,512]{2,1,0:T(8,128)(2,1)S(1)}, bf16[2,512,512]{2,1,0:T(8,128)(2,1)}, u32[]{:S(2)}, u32[]{:S(2)}) collective-permute-start(bf16[2,512,512]{2,1,0:T(8,128)(2,1)S(1)} %get-tuple-element.21), channel_id=1, source_target_pairs={{0,4},{4,0},{8,12},{12,8},{1,5},{5,1},{9,13},{13,9},{2,6},{6,2},{1... | collective-permute-start | bytes 3145736 | tf_op jit(solution)/shard_map/ppermute | solution.py:193
  20.0 71.5 %collective-permute-start.1 = (bf16[2,512,512]{2,1,0:T(8,128)(2,1)S(1)}, bf16[2,512,512]{2,1,0:T(8,128)(2,1)}, u32[]{:S(2)}, u32[]{:S(2)}) collective-permute-start(bf16[2,512,512]{2,1,0:T(8,128)(2,1)S(1)} %get-tuple-element.23), channel_id=1, source_target_pairs={{0,8},{4,12},{8,0},{12,4},{1,9},{5,13},{9,1},{13,5},{2,10},{6,14},... | collective-permute-start | bytes 3145736 | tf_op jit(solution)/shard_map/ppermute | solution.py:193
  23.0 90.6 %collective-permute-start.2 = (bf16[2,512,512]{2,1,0:T(8,128)(2,1)S(1)}, bf16[2,512,512]{2,1,0:T(8,128)(2,1)}, u32[]{:S(2)}, u32[]{:S(2)}) collective-permute-start(bf16[2,512,512]{2,1,0:T(8,128)(2,1)S(1)} %get-tuple-element.20), channel_id=1, source_target_pairs={{0,12},{4,8},{8,4},{12,0},{1,13},{5,9},{9,5},{13,1},{2,14},{6,10},... | collective-permute-start | bytes 3145736 | tf_op jit(solution)/shard_map/ppermute | solution.py:193
  28.0 85.6 %copy-start.1 = (bf16[1,2,64,512]{3,2,1,0:T(8,128)(2,1)S(1)}, bf16[1,2,64,512]{3,2,1,0:T(8,128)(2,1)}, u32[]{:S(2)}) copy-start(bf16[1,2,64,512]{3,2,1,0:T(8,128)(2,1)} %param.10) | copy-start | bytes 393220
  28.0 85.6 %copy-start.2 = (bf16[512,128]{1,0:T(8,128)(2,1)S(1)}, bf16[512,128]{1,0:T(8,128)(2,1)}, u32[]{:S(2)}) copy-start(bf16[512,128]{1,0:T(8,128)(2,1)} %broadcast_11_ones_ref_rest_6_.2.ones_ref.rest_6_) | copy-start | bytes 393220
  113.7 1.0 copy-start
  114.7 1.2 copy-start.3
  163.2 0.7 copy-start.5
Sparse Core Ops, SparseCore 0:
  163.4 35.1 reduce-scatter.1

commit v3 on v2

--- a/solution.py
+++ b/solution.py
@@ -111,10 +111,14 @@
     )(n_valid, q, kv, ones)
 
 
-def shared_kernel(kv_heads, n_blocks, flag_ref, q_ref, m_ref, l_ref, acc_ref, *rest):
+def shared_kernel(kv_heads, n_blocks, with_tree, flag_ref, q_ref, m_ref, l_ref, acc_ref, *rest):
     blocks = rest[:n_blocks]
-    dkv_ref, reach_ref, ones_ref, tree_ones_ref = rest[n_blocks:n_blocks + 4]
-    m_out, l_out, acc_out = rest[n_blocks + 4:n_blocks + 7]
+    ones_ref = rest[n_blocks]
+    rest = rest[n_blocks + 1:]
+    if with_tree:
+        dkv_ref, reach_ref, tree_ones_ref = rest[:3]
+        rest = rest[3:]
+    m_out, l_out, acc_out = rest[:3]
     for h in range(kv_heads):
         cols_h = slice(h * HD, (h + 1) * HD)
         q = q_ref[h]
@@ -127,30 +131,35 @@
         l_out[h] = l
         acc_out[h] = acc
 
-    @pl.when(flag_ref[0] == 1)
-    def _():
-        ok = reach_ref[...] > 0.5
-        for h in range(kv_heads):
-            cols_h = slice(h * HD, (h + 1) * HD)
-            m, l, acc = step(
-                m_out[h], l_out[h], acc_out[h], q_ref[h],
-                dkv_ref[0, :, cols_h], dkv_ref[1, :, cols_h], tree_ones_ref[...], ok,
-            )
-            m_out[h] = m
-            l_out[h] = l
-            acc_out[h] = acc
-
-
-def shared_attend(q, state, blocks, draft_kv, reach_rows, flag):
+    if with_tree:
+        @pl.when(flag_ref[0] == 1)
+        def _():
+            ok = reach_ref[...] > 0.5
+            for h in range(kv_heads):
+                cols_h = slice(h * HD, (h + 1) * HD)
+                m, l, acc = step(
+                    m_out[h], l_out[h], acc_out[h], q_ref[h],
+                    dkv_ref[0, :, cols_h], dkv_ref[1, :, cols_h], tree_ones_ref[...], ok,
+                )
+                m_out[h] = m
+                l_out[h] = l
+                acc_out[h] = acc
+
+
+def shared_attend(q, state, blocks, tree=None):
     kv_heads, rows, _ = q.shape
     n_blocks = len(blocks)
     whole = lambda a: pl.BlockSpec(a.shape, lambda i, f: (0,) * a.ndim)
     ones = jnp.ones((blocks[0].shape[1], HD), jnp.bfloat16)
-    tree_ones = jnp.ones((draft_kv.shape[1], HD), jnp.bfloat16)
-    operands = (q,) + tuple(state) + tuple(blocks) + (draft_kv, reach_rows, ones, tree_ones)
+    operands = (q,) + tuple(state) + tuple(blocks) + (ones,)
+    if tree is not None:
+        draft_kv, reach_rows, flag = tree
+        operands += (draft_kv, reach_rows, jnp.ones((draft_kv.shape[1], HD), jnp.bfloat16))
+    else:
+        flag = jnp.zeros((1,), jnp.int32)
     keys = sum(b.shape[1] for b in blocks)
     return pl.pallas_call(
-        functools.partial(shared_kernel, kv_heads, n_blocks),
+        functools.partial(shared_kernel, kv_heads, n_blocks, tree is not None),
         out_shape=tuple(jax.ShapeDtypeStruct(s.shape, s.dtype) for s in state),
         grid_spec=pltpu.PrefetchScalarGridSpec(
             num_scalar_prefetch=1,
@@ -228,7 +237,10 @@
     reach = tree_reach(parents[0])
     reach_rows = jnp.tile(reach.astype(jnp.float32), (QPK, 1))
     flag = (seq_index == 0).astype(jnp.int32).reshape(1)
-    m, l, acc = shared_attend(queries, state, blocks, draft_kv[0], reach_rows, flag)
+    state = shared_attend(queries, state, blocks[:1], (draft_kv[0], reach_rows, flag))
+    for blk in blocks[1:]:
+        state = shared_attend(queries, state, [blk])
+    m, l, acc = state
 
     heads_dev = kv_heads * QPK
     share = heads_dev // seq_count

time: 208 us -> 197 us (0.947)
  Pallas kernels: 74.8 us -> 29.5 us
  waiting for transfers between devices: 61.5 us -> 91.2 us
  local copies, waits for them, and re-layouts: 12.8 us -> 16.1 us
    pallas_call x1, Pallas kernels: 57.5 us -> 7.91 us  [own_attend(): pl.pallas_call(functools.partial(own_kernel, kv_heads, block), out_shape=...]
    ppermute x3, waiting for transfers between devices: 28.1 us -> 57.8 us  [exchange_shared(): received.append(lax.ppermute(sent, 'req', pairs))]
    pallas_call x1 -> x4, Pallas kernels: 17.4 us -> 21.6 us  [shared_attend(): pl.pallas_call(functools.partial(shared_kernel, kv_heads, n_blocks, tree...]
    unnamed x14 -> x26, local copies, waits for them, and re-layouts: 4.5 us -> 7.3 us
  transfers between devices with their start and end apart: 4 -> 4, of which waited for: 3 -> 4; matrix products, arithmetic and copies ran while one was open for 3% -> 2% of each run, Pallas kernels for 28% -> 13%
where the time goes in v3:
time: 197 us; the launch traced here: 195 us
  waiting for transfers between devices  91.2 us (46%)
  Pallas kernels  29.5 us (15%)
  between operations  22.7 us (12%)
  blocking collectives  18.4 us (9%)
  local copies, waits for them, and re-layouts  16.1 us (8%)
  matrix products  10.9 us (6%)
  starting transfers between devices  3.53 us (2%)
  other arithmetic  2.28 us (1%)
    ppermute x3, waiting for transfers between devices, exchange_shared(): received.append(lax.ppermute(sent, 'req', pairs))  57.8 us
    reduce_scatter x1, waiting for transfers between devices, shards(): lax.psum_scatter(lax.dot_general(out_weight, attended, (((0,), (1,)), (()...  33.4 us
    pallas_call x4, Pallas kernels, shared_attend(): pl.pallas_call(functools.partial(shared_kernel, kv_heads, n_blocks, tree...  21.6 us
    all_to_all x1, blocking collectives, shards(): packed = lax.all_to_all(packed, 'seq', 0, 0, tiled=True)  18.4 us
    dot_general x1, matrix products, shards(): lax.dot_general(out_weight, attended, (((0,), (1,)), ((), ())), preferred...  9.84 us
    pallas_call x1, Pallas kernels, own_attend(): pl.pallas_call(functools.partial(own_kernel, kv_heads, block), out_shape=...  7.91 us
    unnamed x26, local copies, waits for them, and re-layouts  7.3 us
    squeeze x1, local copies, waits for them, and re-layouts, exchange_shared(): lax.dynamic_index_in_dim(shared_cache, group_ids[dst], 1, keepdims=False)  3.99 us
  transfers between devices with their start and end apart: 4, of which 4 were waited for; matrix products, arithmetic and copies ran while one was open for 2% of the time, Pallas kernels for 13%

profile of v3, /device:TPU:8, one launch (start us, length us, event | category | flops | bytes accessed | tf_op | source)
XLA Modules:
  0.0 194.6 jit_solution(3421994308514703943)
XLA Ops:
  7.2 0.0 reduce-scatter.2.cloned.1.call-start
  7.2 1.5 fusion.19
  16.5 0.0 copy-start.9
  16.5 4.0 %dynamic-slice_bitcast_fusion = (bf16[2,512,512]{2,1,0:T(8,128)(2,1)S(1)}, bf16[2,512,512]{2,1,0:T(8,128)(2,1)}, bf16[2,512,512]{2,1,0:T(8,128)(2,1)}, bf16[2,512,512]{2,1,0:T(8,128)(2,1)}) fusion(bf16[2,2,512,512]{3,2,1,0:T(8,128)(2,1)} %param.12, s32[]{:T(128)S(6)} %select_n.59, s32[]{:T(128)S(6)} %select_n.55, s32[]{:T(128)S(6)} %select_n.53, s32[]{:T(128)S(6)} %select_n.57), kind=kLoop, calls=%fused_computation.16 | loop fusion | bytes 8388624 | tf_op jit(solution)/shard_map/jit(dynamic_index_in_dim)/squeeze | solution.py:201
  20.5 0.0 copy-start.10
  20.5 0.0 collective-permute-start
  20.5 3.0 %collective-permute-start.1 = (bf16[2,512,512]{2,1,0:T(8,128)(2,1)}, bf16[2,512,512]{2,1,0:T(8,128)(2,1)}, u32[]{:S(2)}, u32[]{:S(2)}) collective-permute-start(bf16[2,512,512]{2,1,0:T(8,128)(2,1)} %get-tuple-element.41), channel_id=1, source_target_pairs={{0,8},{4,12},{8,0},{12,4},{1,9},{5,13},{9,1},{13,5},{2,10},{6,14},... | collective-permute-start | bytes 3145736 | tf_op jit(solution)/shard_map/ppermute | solution.py:202
  23.5 0.5 collective-permute-start.2
  24.0 0.0 copy-done.9
  24.0 0.1 copy.28
  24.1 1.0 copy.18
  25.8 0.0 copy-done.10
  25.8 0.2 convolution_minimum_fusion.5
  26.0 0.2 convolution_minimum_fusion.4
  26.2 0.2 convolution_minimum_fusion.3
  26.4 0.2 convolution_minimum_fusion.2
  26.6 0.2 convolution_minimum_fusion.1
  26.7 0.2 fusion.2
  26.9 0.7 broadcast_11_ones_ref_rest_1_.2.ones_ref.rest_1_
  27.6 0.0 copy-start
  27.6 0.0 copy-start.1
  27.6 0.0 copy-start.7
  27.6 7.9 %shard_map.104 = (f32[4,512,1]{2,1,0:T(8,128)}, f32[4,512,128]{2,1,0:T(8,128)}, f32[4,512,128]{2,1,0:T(8,128)}) custom-call(s32[1]{0:T(128)} %bitcast.5.nv_ref, bf16[4,512,128]{2,1,0:T(8,128)(2,1)} %bitcast.91, bf16[2,8192,512]{2,1,0:T(8,128)(2,1)} %bitcast.107, bf16[512,128]{1,0:T(8,128)(2,1)} %broadcast_11_ones_ref_rest_1_.2.ones_ref.rest_1_), custom_call_target="tpu_custom_call" | custom-call | flops 12884901888 | bytes 17301504 | tf_op jit(solution)/shard_map/pallas_call | solution.py:91
  35.5 0.0 copy-done
  35.5 0.0 copy-done.1
  35.5 0.0 copy-done.7
  35.5 0.0 copy-start.6
  35.6 1.2 copy-done.6
  36.8 7.1 %shard_map.105 = (f32[4,512,1]{2,1,0:T(8,128)S(1)}, f32[4,512,128]{2,1,0:T(8,128)S(1)}, f32[4,512,128]{2,1,0:T(8,128)S(1)}) custom-call(s32[1]{0:T(128)} %bitcast.3.flag_ref, bf16[4,512,128]{2,1,0:T(8,128)(2,1)S(1)} %bitcast.92, f32[4,512,1]{2,1,0:T(8,128)S(1)} %copy-done.6, f32[4,512,128]{2,1,0:T(8,128)} %get-tuple-element.18.l_ref, ...), custom_call_target="tpu_custom_call" | custom-call | flops 805306368 | bytes 1572864 | tf_op jit(solution)/shard_map/pallas_call | solution.py:161
  43.9 0.0 copy-start.2
  43.9 1.0 copy-done.2
  44.8 20.4 %collective-permute-done.rest_0_ = bf16[2,512,512]{2,1,0:T(8,128)(2,1)} collective-permute-done((bf16[2,512,512]{2,1,0:T(8,128)(2,1)}, bf16[2,512,512]{2,1,0:T(8,128)(2,1)}, u32[]{:S(2)}, u32[]{:S(2)}) %collective-permute-start) | collective-permute-done | bytes 1048608 | tf_op jit(solution)/shard_map/ppermute | solution.py:202
  65.3 4.8 %shard_map.106 = (f32[4,512,1]{2,1,0:T(8,128)S(1)}, f32[4,512,128]{2,1,0:T(8,128)S(1)}, f32[4,512,128]{2,1,0:T(8,128)S(1)}) custom-call(s32[1]{0:T(128)} %constant.18.clone.1.flag_ref, bf16[4,512,128]{2,1,0:T(8,128)(2,1)S(1)} %bitcast.93, f32[4,512,1]{2,1,0:T(8,128)S(1)} %get-tuple-element.20.m_ref, f32[4,512,128]{2,1,0:T(8,128)S(1)} %get-tuple-element.21.l_ref, ...), custom_call_target="tpu_custom_call" | custom-call | flops 805306368 | bytes 1572864 | tf_op jit(solution)/shard_map/pallas_call | solution.py:161
  70.1 0.0 copy-start.4
  70.1 1.0 copy-done.4
  71.1 21.3 %collective-permute-done.1.rest_0_ = bf16[2,512,512]{2,1,0:T(8,128)(2,1)} collective-permute-done((bf16[2,512,512]{2,1,0:T(8,128)(2,1)}, bf16[2,512,512]{2,1,0:T(8,128)(2,1)}, u32[]{:S(2)}, u32[]{:S(2)}) %collective-permute-start.1) | collective-permute-done | bytes 1048608 | tf_op jit(solution)/shard_map/ppermute | solution.py:202
  92.4 4.9 %shard_map.107 = (f32[4,512,1]{2,1,0:T(8,128)S(1)}, f32[4,512,128]{2,1,0:T(8,128)S(1)}, f32[4,512,128]{2,1,0:T(8,128)S(1)}) custom-call(s32[1]{0:T(128)} %constant.18.clone.1.flag_ref, bf16[4,512,128]{2,1,0:T(8,128)(2,1)S(1)} %bitcast.94, f32[4,512,1]{2,1,0:T(8,128)S(1)} %get-tuple-element.23.m_ref, f32[4,512,128]{2,1,0:T(8,128)S(1)} %get-tuple-element.24.l_ref, ...), custom_call_target="tpu_custom_call" | custom-call | flops 805306368 | bytes 1572864 | tf_op jit(solution)/shard_map/pallas_call | solution.py:161
  97.2 0.0 copy-start.3
  97.2 1.0 copy-done.3
  98.2 16.1 %collective-permute-done.2.rest_0_ = bf16[2,512,512]{2,1,0:T(8,128)(2,1)S(1)} collective-permute-done((bf16[2,512,512]{2,1,0:T(8,128)(2,1)S(1)}, bf16[2,512,512]{2,1,0:T(8,128)(2,1)S(1)}, u32[]{:S(2)}, u32[]{:S(2)}) %collective-permute-start.2) | collective-permute-done | bytes 1048608 | tf_op jit(solution)/shard_map/ppermute | solution.py:202
  114.3 0.0 copy-start.8
  114.3 1.0 copy-done.8
  115.3 4.8 %shard_map.108 = (f32[4,512,1]{2,1,0:T(8,128)S(1)}, f32[4,512,128]{2,1,0:T(8,128)S(1)}, f32[4,512,128]{2,1,0:T(8,128)S(1)}) custom-call(s32[1]{0:T(128)} %constant.18.clone.1.flag_ref, bf16[4,512,128]{2,1,0:T(8,128)(2,1)S(1)} %bitcast.95, f32[4,512,1]{2,1,0:T(8,128)S(1)} %get-tuple-element.26.m_ref, f32[4,512,128]{2,1,0:T(8,128)S(1)} %get-tuple-element.27.l_ref, ...), custom_call_target="tpu_custom_call" | custom-call | flops 805306368 | bytes 1572864 | tf_op jit(solution)/shard_map/pallas_call | solution.py:161
  120.1 0.0 copy-start.5
  120.2 1.0 copy-done.5
  121.1 1.6 reduce.1
  122.7 0.1 reshape_squeeze.10
  122.8 0.4 slice_reduce_fusion
  123.1 0.1 reshape_squeeze.11
  123.2 0.1 pad_maximum_fusion.1
  123.3 0.1 pad_maximum_fusion
  123.4 18.4 %all_to_all.5 = f32[32,65,128]{2,1,0:T(8,128)S(1)} all-to-all(f32[32,65,128]{2,1,0:T(8,128)S(1)} %pad_maximum_fusion), channel_id=1, replica_groups=mesh['tensor'=2,'req'=4,'seq'=4] {'seq'}, dimensions={0} | all-to-all | bytes 2129920 | tf_op jit(solution)/shard_map/all_to_all | solution.py:253
  141.8 0.2 copy.43
  142.0 0.1 fusion.13
  142.1 0.1 copy.21
  142.2 0.3 fusion.3
  142.5 9.8 %fusion = bf16[8192,64]{0,1:T(8,128)(2,1)} fusion(bf16[1024,8192]{1,0:T(8,128)(2,1)} %param.13, f32[64,8]{0,1:T(8,128)S(1)} %bitcast.105, f32[8,64,128]{2,0,1:T(8,128)S(1)} %fusion.3), kind=kOutput, calls=%fused_computation.2 | convolution fusion | flops 1074397184 | bytes 18089984 | tf_op jit(solution)/shard_map/dot_general | solution.py:265
  152.4 0.0 reduce-scatter.2.cloned.1.call-update
  152.4 0.1 copy.24
  152.6 0.5 copy-done.11
  153.1 0.6 gather_fusion
  153.7 0.1 broadcast_select_fusion
  153.8 0.6 copy.25
  154.4 33.4 %reduce-scatter.2.cloned.1.call-done = bf16[1024,64]{0,1:T(8,128)(2,1)} async-done(((bf16[8192,64]{0,1:T(8,128)(2,1)}), bf16[1024,64]{0,1:T(8,128)(2,1)}) %reduce-scatter.2.cloned.1.call-update) | async-done | bytes 131088 | tf_op jit(solution)/shard_map/reduce_scatter | solution.py:264
  (7 shorter events, 0.1 us)
Async XLA Ops:
  7.2 180.6 %reduce-scatter.2.cloned.1.call-start = ((), (), s32[]{:S(2)}) async-start(), calls=%async_computation.2 | async-start | bytes 1179648 | tf_op jit(solution)/shard_map/reduce_scatter | solution.py:264
  16.5 7.5 %copy-start.9 = (bf16[1,64,4096]{2,1,0:T(8,128)(2,1)S(1)}, bf16[1,64,4096]{2,1,0:T(8,128)(2,1)}, u32[]{:S(2)}) copy-start(bf16[1,64,4096]{2,1,0:T(8,128)(2,1)} %param.9) | copy-start | bytes 1572868
  20.5 5.3 %copy-start.10 = (s32[1,64]{1,0:T(1,128)S(1)}, s32[1,64]{1,0:T(1,128)}, u32[]{:S(2)}) copy-start(s32[1,64]{1,0:T(1,128)} %param.16) | copy-start | bytes 772
  20.5 44.7 %collective-permute-start = (bf16[2,512,512]{2,1,0:T(8,128)(2,1)}, bf16[2,512,512]{2,1,0:T(8,128)(2,1)}, u32[]{:S(2)}, u32[]{:S(2)}) collective-permute-start(bf16[2,512,512]{2,1,0:T(8,128)(2,1)} %get-tuple-element.39), channel_id=1, source_target_pairs={{0,4},{4,0},{8,12},{12,8},{1,5},{5,1},{9,13},{13,9},{2,6},{6,2},{1... | collective-permute-start | bytes 3145736 | tf_op jit(solution)/shard_map/ppermute | solution.py:202
  20.5 71.8 %collective-permute-start.1 = (bf16[2,512,512]{2,1,0:T(8,128)(2,1)}, bf16[2,512,512]{2,1,0:T(8,128)(2,1)}, u32[]{:S(2)}, u32[]{:S(2)}) collective-permute-start(bf16[2,512,512]{2,1,0:T(8,128)(2,1)} %get-tuple-element.41), channel_id=1, source_target_pairs={{0,8},{4,12},{8,0},{12,4},{1,9},{5,13},{9,1},{13,5},{2,10},{6,14},... | collective-permute-start | bytes 3145736 | tf_op jit(solution)/shard_map/ppermute | solution.py:202
  23.5 90.7 %collective-permute-start.2 = (bf16[2,512,512]{2,1,0:T(8,128)(2,1)S(1)}, bf16[2,512,512]{2,1,0:T(8,128)(2,1)S(1)}, u32[]{:S(2)}, u32[]{:S(2)}) collective-permute-start(bf16[2,512,512]{2,1,0:T(8,128)(2,1)S(1)} %get-tuple-element.38), channel_id=1, source_target_pairs={{0,12},{4,8},{8,4},{12,0},{1,13},{5,9},{9,5},{13,1},{2,14},{6,10},... | collective-permute-start | bytes 3145736 | tf_op jit(solution)/shard_map/ppermute | solution.py:202
  27.6 8.0 %copy-start = (bf16[64,4,8,128]{3,0,2,1:T(8,128)(2,1)S(1)}, bf16[64,4,8,128]{3,0,2,1:T(8,128)(2,1)}, u32[]{:S(2)}) copy-start(bf16[64,4,8,128]{3,0,2,1:T(8,128)(2,1)} %copy.18) | copy-start | bytes 1572868
  27.6 8.0 %copy-start.1 = (bf16[512,128]{1,0:T(8,128)(2,1)S(1)}, bf16[512,128]{1,0:T(8,128)(2,1)}, u32[]{:S(2)}) copy-start(bf16[512,128]{1,0:T(8,128)(2,1)} %broadcast_11_ones_ref_rest_1_.2.ones_ref.rest_1_) | copy-start | bytes 393220
  27.6 8.0 %copy-start.7 = (bf16[1,2,64,512]{3,2,1,0:T(8,128)(2,1)S(1)}, bf16[1,2,64,512]{3,2,1,0:T(8,128)(2,1)}, u32[]{:S(2)}) copy-start(bf16[1,2,64,512]{3,2,1,0:T(8,128)(2,1)} %param.10) | copy-start | bytes 393220
  35.5 1.2 copy-start.6
  43.9 1.0 copy-start.2
  70.1 1.0 copy-start.4
  97.2 1.0 copy-start.3
  114.3 1.0 copy-start.8
  120.1 1.0 copy-start.5
  152.4 0.7 copy-start.11
Sparse Core Ops, SparseCore 0:
  152.5 35.1 reduce-scatter.1

commit v4 on v3

--- a/solution.py
+++ b/solution.py
@@ -261,15 +261,17 @@
     final_sum = jnp.sum(part_sum * factor[..., None], axis=0)
     attended = (final_sum / final_total[..., None]).astype(jnp.bfloat16)
     attended = jnp.transpose(attended, (1, 0, 2)).reshape(draft_len, share * HD)
-    out_piece = lax.psum_scatter(
-        lax.dot_general(
-            out_weight, attended, (((0,), (1,)), ((), ())), preferred_element_type=jnp.float32
-        ).astype(jnp.bfloat16),
-        ("tensor", "seq"),
-        scatter_dimension=0,
-        tiled=True,
-    )
-    verified = out_piece.T[None]
+    out_group = ("tensor", "seq")
+    owners = lax.axis_size("tensor") * seq_count
+    columns = out_weight.shape[1] // owners
+    product = jnp.einsum(
+        "ik,kcj->cij",
+        attended,
+        out_weight.reshape(out_weight.shape[0], owners, columns),
+        preferred_element_type=jnp.float32,
+    ).astype(jnp.bfloat16)
+    pieces = lax.all_to_all(product, out_group, 0, 0, tiled=True)
+    verified = jnp.sum(pieces.astype(jnp.float32), axis=0).astype(jnp.bfloat16)[None]
     accepted_kv = jnp.take(draft_kv[0], accepted[0], axis=1)[None]
     return (verified, accepted_kv)
 

time: 197 us -> 165 us (0.84)
  waiting for transfers between devices: 91.2 us -> 22 us
  Pallas kernels: 29.5 us -> 79.2 us
  between operations: 22.7 us -> 9.21 us
  starting transfers between devices: 3.53 us -> 7.18 us
    ppermute x3, waiting for transfers between devices: 57.8 us -> 8.13 us  [exchange_shared(): received.append(lax.ppermute(sent, 'req', pairs))]
    pallas_call x1, Pallas kernels: 7.91 us -> 57.5 us  [own_attend(): pl.pallas_call(functools.partial(own_kernel, kv_heads, block), out_shape=...]
    reduce_scatter x1 -> x0, waiting for transfers between devices: 33.4 us -> none  [shards(): lax.psum_scatter(lax.dot_general(out_weight, attended, (((0,), (1,)), (()...]
    all_to_all x0 -> x1, waiting for transfers between devices: none -> 13.8 us  [shards(): pieces = lax.all_to_all(product, out_group, 0, 0, tiled=True)]
    all_to_all x0 -> x1, starting transfers between devices: none -> 3.69 us  [shards(): pieces = lax.all_to_all(product, out_group, 0, 0, tiled=True)]
  transfers between devices with their start and end apart: 4 -> 4, of which waited for: 4 -> 2; matrix products, arithmetic and copies ran while one was open for 2% -> 3% of each run, Pallas kernels for 13% -> 45%
where the time goes in v4:
time: 165 us; the launch traced here: 164 us
  Pallas kernels  79.2 us (48%)
  waiting for transfers between devices  22 us (13%)
  blocking collectives  18.4 us (11%)
  local copies, waits for them, and re-layouts  15.7 us (10%)
  matrix products  9.46 us (6%)
  between operations  9.21 us (6%)
  starting transfers between devices  7.18 us (4%)
  other arithmetic  3.28 us (2%)
    pallas_call x1, Pallas kernels, own_attend(): pl.pallas_call(functools.partial(own_kernel, kv_heads, block), out_shape=...  57.5 us
    pallas_call x4, Pallas kernels, shared_attend(): pl.pallas_call(functools.partial(shared_kernel, kv_heads, n_blocks, tree...  21.6 us
    all_to_all x1, blocking collectives, shards(): packed = lax.all_to_all(packed, 'seq', 0, 0, tiled=True)  18.4 us
    all_to_all x1, waiting for transfers between devices, shards(): pieces = lax.all_to_all(product, out_group, 0, 0, tiled=True)  13.8 us
    dot_general x1, matrix products, shards(): jnp.einsum('ik,kcj->cij', attended, out_weight.reshape(out_weight.shape[0...  8.41 us
    ppermute x3, waiting for transfers between devices, exchange_shared(): received.append(lax.ppermute(sent, 'req', pairs))  8.13 us
    unnamed x26, local copies, waits for them, and re-layouts  6.83 us
    squeeze x1, local copies, waits for them, and re-layouts, exchange_shared(): lax.dynamic_index_in_dim(shared_cache, group_ids[dst], 1, keepdims=False)  3.99 us
  transfers between devices with their start and end apart: 4, of which 2 were waited for; matrix products, arithmetic and copies ran while one was open for 3% of the time, Pallas kernels for 45%

profile of v4, /device:TPU:8, one launch (start us, length us, event | category | flops | bytes accessed | tf_op | source)
XLA Modules:
  0.0 164.4 jit_solution(5442285071520145349)
XLA Ops:
  0.6 1.5 fusion.24
  9.7 0.0 copy-start.9
  9.7 4.0 %dynamic-slice_bitcast_fusion = (bf16[2,512,512]{2,1,0:T(8,128)(2,1)S(1)}, bf16[2,512,512]{2,1,0:T(8,128)(2,1)}, bf16[2,512,512]{2,1,0:T(8,128)(2,1)}, bf16[2,512,512]{2,1,0:T(8,128)(2,1)}) fusion(bf16[2,2,512,512]{3,2,1,0:T(8,128)(2,1)} %param.12, s32[]{:T(128)S(6)} %select_n.59, s32[]{:T(128)S(6)} %select_n.55, s32[]{:T(128)S(6)} %select_n.53, s32[]{:T(128)S(6)} %select_n.57), kind=kLoop, calls=%fused_computation.19 | loop fusion | bytes 8388624 | tf_op jit(solution)/shard_map/jit(dynamic_index_in_dim)/squeeze | solution.py:201
  13.7 0.0 copy-start.10
  13.7 0.0 collective-permute-start
  13.7 3.0 %collective-permute-start.1 = (bf16[2,512,512]{2,1,0:T(8,128)(2,1)}, bf16[2,512,512]{2,1,0:T(8,128)(2,1)}, u32[]{:S(2)}, u32[]{:S(2)}) collective-permute-start(bf16[2,512,512]{2,1,0:T(8,128)(2,1)} %get-tuple-element.43), channel_id=1, source_target_pairs={{0,8},{4,12},{8,0},{12,4},{1,9},{5,13},{9,1},{13,5},{2,10},{6,14},... | collective-permute-start | bytes 3145736 | tf_op jit(solution)/shard_map/ppermute | solution.py:202
  16.8 0.5 collective-permute-start.2
  17.2 0.0 copy-done.9
  17.2 0.1 copy.39
  17.3 1.0 copy.28
  19.0 0.0 copy-done.10
  19.0 0.2 convolution_minimum_fusion.5
  19.3 0.2 convolution_minimum_fusion.4
  19.4 0.2 convolution_minimum_fusion.3
  19.6 0.2 convolution_minimum_fusion.2
  19.8 0.2 convolution_minimum_fusion.1
  20.0 0.2 fusion.10
  20.1 0.7 broadcast_11_ones_ref_rest_1_.2.ones_ref.rest_1_
  20.8 0.0 copy-start
  20.8 57.5 %shard_map.104 = (f32[4,512,1]{2,1,0:T(8,128)}, f32[4,512,128]{2,1,0:T(8,128)}, f32[4,512,128]{2,1,0:T(8,128)}) custom-call(s32[1]{0:T(128)} %bitcast.5.nv_ref, bf16[4,512,128]{2,1,0:T(8,128)(2,1)} %bitcast.86, bf16[2,8192,512]{2,1,0:T(8,128)(2,1)} %bitcast.103, bf16[512,128]{1,0:T(8,128)(2,1)} %broadcast_11_ones_ref_rest_1_.2.ones_ref.rest_1_), custom_call_target="tpu_custom_call" | custom-call | flops 12884901888 | bytes 17301504 | tf_op jit(solution)/shard_map/pallas_call | solution.py:91
  78.4 0.0 copy-done
  78.4 0.0 copy-done.1
  78.4 0.0 copy-done.7
  78.4 0.0 copy-start.6
  78.4 1.2 copy-done.6
  79.6 7.1 %shard_map.105 = (f32[4,512,1]{2,1,0:T(8,128)S(1)}, f32[4,512,128]{2,1,0:T(8,128)S(1)}, f32[4,512,128]{2,1,0:T(8,128)S(1)}) custom-call(s32[1]{0:T(128)} %bitcast.3.flag_ref, bf16[4,512,128]{2,1,0:T(8,128)(2,1)S(1)} %bitcast.87, f32[4,512,1]{2,1,0:T(8,128)S(1)} %copy-done.6, f32[4,512,128]{2,1,0:T(8,128)} %get-tuple-element.18.l_ref, ...), custom_call_target="tpu_custom_call" | custom-call | flops 805306368 | bytes 1572864 | tf_op jit(solution)/shard_map/pallas_call | solution.py:161
  86.7 0.0 copy-start.2
  86.7 1.0 copy-done.2
  87.7 0.0 collective-permute-done.rest_0_
  87.7 4.9 %shard_map.106 = (f32[4,512,1]{2,1,0:T(8,128)S(1)}, f32[4,512,128]{2,1,0:T(8,128)S(1)}, f32[4,512,128]{2,1,0:T(8,128)S(1)}) custom-call(s32[1]{0:T(128)} %constant.17.clone.1.flag_ref, bf16[4,512,128]{2,1,0:T(8,128)(2,1)S(1)} %bitcast.88, f32[4,512,1]{2,1,0:T(8,128)S(1)} %get-tuple-element.20.m_ref, f32[4,512,128]{2,1,0:T(8,128)S(1)} %get-tuple-element.21.l_ref, ...), custom_call_target="tpu_custom_call" | custom-call | flops 805306368 | bytes 1572864 | tf_op jit(solution)/shard_map/pallas_call | solution.py:161
  92.5 0.0 copy-start.4
  92.5 1.0 copy-done.4
  93.5 0.0 collective-permute-done.1.rest_0_
  93.5 4.8 %shard_map.107 = (f32[4,512,1]{2,1,0:T(8,128)S(1)}, f32[4,512,128]{2,1,0:T(8,128)S(1)}, f32[4,512,128]{2,1,0:T(8,128)S(1)}) custom-call(s32[1]{0:T(128)} %constant.17.clone.1.flag_ref, bf16[4,512,128]{2,1,0:T(8,128)(2,1)S(1)} %bitcast.89, f32[4,512,1]{2,1,0:T(8,128)S(1)} %get-tuple-element.23.m_ref, f32[4,512,128]{2,1,0:T(8,128)S(1)} %get-tuple-element.24.l_ref, ...), custom_call_target="tpu_custom_call" | custom-call | flops 805306368 | bytes 1572864 | tf_op jit(solution)/shard_map/pallas_call | solution.py:161
  98.4 0.0 copy-start.3
  98.4 1.0 copy-done.3
  99.4 8.1 %collective-permute-done.2.rest_0_ = bf16[2,512,512]{2,1,0:T(8,128)(2,1)S(1)} collective-permute-done((bf16[2,512,512]{2,1,0:T(8,128)(2,1)S(1)}, bf16[2,512,512]{2,1,0:T(8,128)(2,1)S(1)}, u32[]{:S(2)}, u32[]{:S(2)}) %collective-permute-start.2) | collective-permute-done | bytes 1048608 | tf_op jit(solution)/shard_map/ppermute | solution.py:202
  107.5 1.0 copy-done.8
  108.5 4.8 %shard_map.108 = (f32[4,512,1]{2,1,0:T(8,128)S(1)}, f32[4,512,128]{2,1,0:T(8,128)S(1)}, f32[4,512,128]{2,1,0:T(8,128)S(1)}) custom-call(s32[1]{0:T(128)} %constant.17.clone.1.flag_ref, bf16[4,512,128]{2,1,0:T(8,128)(2,1)S(1)} %bitcast.90, f32[4,512,1]{2,1,0:T(8,128)S(1)} %get-tuple-element.26.m_ref, f32[4,512,128]{2,1,0:T(8,128)S(1)} %get-tuple-element.27.l_ref, ...), custom_call_target="tpu_custom_call" | custom-call | flops 805306368 | bytes 1572864 | tf_op jit(solution)/shard_map/pallas_call | solution.py:161
  113.4 0.0 copy-start.5
  113.4 1.0 copy-done.5
  114.3 1.6 reduce.2
  115.9 0.1 reshape_squeeze.10
  116.0 0.4 slice_reduce_fusion
  116.3 0.1 reshape_squeeze.11
  116.4 0.1 pad_maximum_fusion.1
  116.5 0.1 pad_maximum_fusion
  116.6 18.4 %all_to_all.10 = f32[32,65,128]{2,1,0:T(8,128)S(1)} all-to-all(f32[32,65,128]{2,1,0:T(8,128)S(1)} %pad_maximum_fusion), channel_id=1, replica_groups=mesh['tensor'=2,'req'=4,'seq'=4] {'seq'}, dimensions={0} | all-to-all | bytes 2129920 | tf_op jit(solution)/shard_map/all_to_all | solution.py:253
  135.0 0.2 copy.54
  135.2 0.1 fusion.18
  135.3 0.1 copy.31
  135.4 0.4 fusion.11
  135.8 0.1 fusion.13
  135.9 0.1 copy.33
  136.0 0.1 reshape.104
  136.1 8.4 %fusion.6 = bf16[8,64,1024]{2,1,0:T(8,128)(2,1)} fusion(bf16[64,1024,1]{1,0,2:T(8,128)(2,1)S(1)} %reshape.104, bf16[128,8,8,1024]{3,2,1,0:T(8,128)(2,1)} %bitcast.104), kind=kOutput, calls=%fused_computation.5 | convolution fusion | flops 1074266112 | bytes 17956864 | tf_op jit(solution)/shard_map/ik,kcj->cij/dot_general | solution.py:267
  144.5 3.7 %all-to-all-start.1 = ((bf16[8,64,1024]{2,1,0:T(8,128)(2,1)}), bf16[8,64,1024]{2,1,0:T(8,128)(2,1)S(1)}, u32[]{:S(2)}, u32[]{:S(2)}) async-start(bf16[8,64,1024]{2,1,0:T(8,128)(2,1)} %fusion.6), calls=%async_computation.1 | async-start | bytes 2097152 | tf_op jit(solution)/shard_map/all_to_all | solution.py:273
  148.2 0.1 copy.35
  148.4 0.0 copy-done.11
  148.4 0.6 gather_fusion
  149.0 0.1 broadcast_select_fusion
  149.1 0.6 copy.36
  149.7 13.8 %all-to-all-done.1 = bf16[8,64,1024]{2,1,0:T(8,128)(2,1)S(1)} async-done(((bf16[8,64,1024]{2,1,0:T(8,128)(2,1)}), bf16[8,64,1024]{2,1,0:T(8,128)(2,1)S(1)}, u32[]{:S(2)}, u32[]{:S(2)}) %all-to-all-start.1) | async-done | bytes 1048608 | tf_op jit(solution)/shard_map/all_to_all | solution.py:273
  163.5 0.8 reduce_sum.35
  (10 shorter events, 0.1 us)
Async XLA Ops:
  9.7 7.5 %copy-start.9 = (bf16[1,64,4096]{2,1,0:T(8,128)(2,1)S(1)}, bf16[1,64,4096]{2,1,0:T(8,128)(2,1)}, u32[]{:S(2)}) copy-start(bf16[1,64,4096]{2,1,0:T(8,128)(2,1)} %param.9) | copy-start | bytes 1572868
  13.7 5.3 %copy-start.10 = (s32[1,64]{1,0:T(1,128)S(1)}, s32[1,64]{1,0:T(1,128)}, u32[]{:S(2)}) copy-start(s32[1,64]{1,0:T(1,128)} %param.16) | copy-start | bytes 772
  13.7 73.9 %collective-permute-start = (bf16[2,512,512]{2,1,0:T(8,128)(2,1)}, bf16[2,512,512]{2,1,0:T(8,128)(2,1)}, u32[]{:S(2)}, u32[]{:S(2)}) collective-permute-start(bf16[2,512,512]{2,1,0:T(8,128)(2,1)} %get-tuple-element.41), channel_id=1, source_target_pairs={{0,4},{4,0},{8,12},{12,8},{1,5},{5,1},{9,13},{13,9},{2,6},{6,2},{1... | collective-permute-start | bytes 3145736 | tf_op jit(solution)/shard_map/ppermute | solution.py:202
  13.7 79.8 %collective-permute-start.1 = (bf16[2,512,512]{2,1,0:T(8,128)(2,1)}, bf16[2,512,512]{2,1,0:T(8,128)(2,1)}, u32[]{:S(2)}, u32[]{:S(2)}) collective-permute-start(bf16[2,512,512]{2,1,0:T(8,128)(2,1)} %get-tuple-element.43), channel_id=1, source_target_pairs={{0,8},{4,12},{8,0},{12,4},{1,9},{5,13},{9,1},{13,5},{2,10},{6,14},... | collective-permute-start | bytes 3145736 | tf_op jit(solution)/shard_map/ppermute | solution.py:202
  16.8 90.7 %collective-permute-start.2 = (bf16[2,512,512]{2,1,0:T(8,128)(2,1)S(1)}, bf16[2,512,512]{2,1,0:T(8,128)(2,1)S(1)}, u32[]{:S(2)}, u32[]{:S(2)}) collective-permute-start(bf16[2,512,512]{2,1,0:T(8,128)(2,1)S(1)} %get-tuple-element.40), channel_id=1, source_target_pairs={{0,12},{4,8},{8,4},{12,0},{1,13},{5,9},{9,5},{13,1},{2,14},{6,10},... | collective-permute-start | bytes 3145736 | tf_op jit(solution)/shard_map/ppermute | solution.py:202
  20.8 57.6 %copy-start = (bf16[64,4,8,128]{3,0,2,1:T(8,128)(2,1)S(1)}, bf16[64,4,8,128]{3,0,2,1:T(8,128)(2,1)}, u32[]{:S(2)}) copy-start(bf16[64,4,8,128]{3,0,2,1:T(8,128)(2,1)} %copy.28) | copy-start | bytes 1572868
  20.8 57.6 %copy-start.1 = (bf16[512,128]{1,0:T(8,128)(2,1)S(1)}, bf16[512,128]{1,0:T(8,128)(2,1)}, u32[]{:S(2)}) copy-start(bf16[512,128]{1,0:T(8,128)(2,1)} %broadcast_11_ones_ref_rest_1_.2.ones_ref.rest_1_) | copy-start | bytes 393220
  20.8 57.6 %copy-start.7 = (bf16[1,2,64,512]{3,2,1,0:T(8,128)(2,1)S(1)}, bf16[1,2,64,512]{3,2,1,0:T(8,128)(2,1)}, u32[]{:S(2)}) copy-start(bf16[1,2,64,512]{3,2,1,0:T(8,128)(2,1)} %param.10) | copy-start | bytes 393220
  78.4 1.2 copy-start.6
  86.7 1.0 copy-start.2
  92.5 1.0 copy-start.4
  98.4 1.0 copy-start.3
  107.5 1.0 copy-start.8
  113.4 1.0 copy-start.5
  144.5 3.8 %copy-start.11 = (s32[1,8]{1,0:T(1,128)S(1)}, s32[1,8]{1,0:T(1,128)}, u32[]{:S(2)}) copy-start(s32[1,8]{1,0:T(1,128)} %param.17) | copy-start | bytes 100
  144.5 19.0 %all-to-all-start.1 = ((bf16[8,64,1024]{2,1,0:T(8,128)(2,1)}), bf16[8,64,1024]{2,1,0:T(8,128)(2,1)S(1)}, u32[]{:S(2)}, u32[]{:S(2)}) async-start(bf16[8,64,1024]{2,1,0:T(8,128)(2,1)} %fusion.6), calls=%async_computation.1 | async-start | bytes 2097152 | tf_op jit(solution)/shard_map/all_to_all | solution.py:273

commit v5 on v4

--- a/solution.py
+++ b/solution.py
@@ -187,9 +187,17 @@
     return reach > 0.5
 
 
+def pick_group(shared_cache, group_ids, request):
+    onehot = jnp.arange(group_ids.shape[0], dtype=jnp.int32) == request
+    group = jnp.sum(jnp.where(onehot, group_ids, 0))
+    picked = shared_cache[:, 0]
+    for g in range(1, shared_cache.shape[1]):
+        picked = jnp.where(group == g, shared_cache[:, g], picked)
+    return picked
+
+
 def exchange_shared(shared_cache, group_ids, req_index, req_count):
-    local = shared_cache[:, group_ids[req_index]]
-    received = [local]
+    received = [pick_group(shared_cache, group_ids, req_index)]
     pow2 = req_count & (req_count - 1) == 0
     for k in range(1, req_count):
         if pow2:
@@ -198,9 +206,19 @@
         else:
             pairs = [(r, (r + k) % req_count) for r in range(req_count)]
             dst = (req_index + k) % req_count
-        sent = lax.dynamic_index_in_dim(shared_cache, group_ids[dst], 1, keepdims=False)
+        sent = pick_group(shared_cache, group_ids, dst)
         received.append(lax.ppermute(sent, "req", pairs))
     return received
+
+
+def split16(x):
+    high = x.astype(jnp.bfloat16)
+    low = (x - high.astype(jnp.float32)).astype(jnp.bfloat16)
+    return high, low
+
+
+def join16(high, low):
+    return high.astype(jnp.float32) + low.astype(jnp.float32)
 
 
 def shards(
@@ -244,20 +262,23 @@
 
     heads_dev = kv_heads * QPK
     share = heads_dev // seq_count
-    stats = jnp.concatenate(
-        [m[..., 0].reshape(heads_dev, draft_len), l[..., 0].reshape(heads_dev, draft_len)], 1
-    )
-    packed = jnp.concatenate(
-        [acc.reshape(heads_dev, draft_len, HD), stats.reshape(heads_dev, 1, 2 * draft_len)], 1
-    )
+    part_out = (acc / l).astype(jnp.bfloat16).reshape(heads_dev, draft_len, HD)
+    m_hi, m_lo = split16(m[..., 0].reshape(heads_dev, draft_len))
+    l_hi, l_lo = split16(l[..., 0].reshape(heads_dev, draft_len))
+    stats = jnp.stack(
+        [jnp.concatenate([m_hi, m_lo], 1), jnp.concatenate([l_hi, l_lo], 1)], 1
+    )
+    packed = jnp.concatenate([part_out, stats], 1)
     packed = lax.all_to_all(packed, "seq", 0, 0, tiled=True)
-    packed = packed.reshape(seq_count, share, draft_len + 1, 2 * draft_len)
-    part_max = packed[:, :, draft_len, :draft_len]
-    part_total = packed[:, :, draft_len, draft_len:]
-    part_sum = packed[:, :, :draft_len, :]
+    packed = packed.reshape(seq_count, share, draft_len + 2, 2 * draft_len)
+    part_max = join16(packed[:, :, draft_len, :draft_len], packed[:, :, draft_len, draft_len:])
+    part_total = join16(
+        packed[:, :, draft_len + 1, :draft_len], packed[:, :, draft_len + 1, draft_len:]
+    )
+    part_sum = packed[:, :, :draft_len, :].astype(jnp.float32)
     final_max = jnp.max(part_max, axis=0)
-    factor = jnp.exp2((part_max - final_max[None]) * EXP2_SCALE)
-    final_total = jnp.sum(part_total * factor, axis=0)
+    factor = jnp.exp2((part_max - final_max[None]) * EXP2_SCALE) * part_total
+    final_total = jnp.sum(factor, axis=0)
     final_sum = jnp.sum(part_sum * factor[..., None], axis=0)
     attended = (final_sum / final_total[..., None]).astype(jnp.bfloat16)
     attended = jnp.transpose(attended, (1, 0, 2)).reshape(draft_len, share * HD)

time: 165 us -> 151 us (0.915)
  blocking collectives: 18.4 us -> 12.1 us
  local copies, waits for them, and re-layouts: 15.7 us -> 10.3 us
  between operations: 9.21 us -> 4.16 us
  other arithmetic: 3.28 us -> 7.54 us
    all_to_all x1, blocking collectives: 18.4 us -> 12.1 us  [shards(): packed = lax.all_to_all(packed, 'seq', 0, 0, tiled=True)]
    squeeze x1 -> x0, local copies, waits for them, and re-layouts: 3.99 us -> none  [exchange_shared(): lax.dynamic_index_in_dim(shared_cache, group_ids[dst], 1, keepdims=False)]
    select_n x0 -> x1, other arithmetic: none -> 3.79 us  [pick_group(): picked = jnp.where(group == g, shared_cache[:, g], picked)]
  transfers between devices with their start and end apart: 4 -> 4, of which waited for: 2 -> 2; matrix products, arithmetic and copies ran while one was open for 3% -> 3% of each run, Pallas kernels for 45% -> 49%
where the time goes in v5:
time: 151 us
  Pallas kernels  79.1 us (52%)
  waiting for transfers between devices  20.9 us (14%)
  blocking collectives  12.1 us (8%)
  local copies, waits for them, and re-layouts  10.3 us (7%)
  matrix products  9.48 us (6%)
  other arithmetic  7.54 us (5%)
  starting transfers between devices  7.18 us (5%)
  between operations  4.16 us (3%)
    pallas_call x1, Pallas kernels, own_attend(): pl.pallas_call(functools.partial(own_kernel, kv_heads, block), out_shape=...  57.5 us
    pallas_call x4, Pallas kernels, shared_attend(): pl.pallas_call(functools.partial(shared_kernel, kv_heads, n_blocks, tree...  21.6 us
    all_to_all x1, waiting for transfers between devices, shards(): pieces = lax.all_to_all(product, out_group, 0, 0, tiled=True)  13.8 us
    all_to_all x1, blocking collectives, shards(): packed = lax.all_to_all(packed, 'seq', 0, 0, tiled=True)  12.1 us
    dot_general x1, matrix products, shards(): jnp.einsum('ik,kcj->cij', attended, out_weight.reshape(out_weight.shape[0...  8.44 us
    ppermute x3, waiting for transfers between devices, exchange_shared(): received.append(lax.ppermute(sent, 'req', pairs))  7.04 us
    unnamed x26, local copies, waits for them, and re-layouts  6.94 us
    select_n x1, other arithmetic, pick_group(): picked = jnp.where(group == g, shared_cache[:, g], picked)  3.79 us
  transfers between devices with their start and end apart: 4, of which 2 were waited for; matrix products, arithmetic and copies ran while one was open for 3% of the time, Pallas kernels for 49%

profile of v5, /device:TPU:8, one launch (start us, length us, event | category | flops | bytes accessed | tf_op | source)
XLA Modules:
  0.0 150.7 jit_solution(5373109955486917246)
XLA Ops:
  0.6 1.4 fusion.27
  4.6 0.0 copy-start.9
  4.6 3.8 %fusion.14 = (bf16[2,512,512]{2,1,0:T(8,128)(2,1)}, bf16[2,512,512]{2,1,0:T(8,128)(2,1)}, bf16[2,512,512]{2,1,0:T(8,128)(2,1)}, bf16[2,512,512]{2,1,0:T(8,128)(2,1)}) fusion(pred[]{:T(512)S(6)} %eq.74, bf16[2,2,512,512]{3,2,1,0:T(8,128)(2,1)} %param.12, pred[]{:T(512)S(6)} %eq.71, pred[]{:T(512)S(6)} %eq.68, pred[]{:T(512)S(6)} %eq.60), kind=kLoop, calls=%fused_computation.21 | loop fusion | flops 2097152 | bytes 6291460 | tf_op jit(solution)/shard_map/jit(_where)/select_n | solution.py:195
  8.4 0.0 collective-permute-start
  8.4 3.0 %collective-permute-start.1 = (bf16[2,512,512]{2,1,0:T(8,128)(2,1)}, bf16[2,512,512]{2,1,0:T(8,128)(2,1)S(1)}, u32[]{:S(2)}, u32[]{:S(2)}) collective-permute-start(bf16[2,512,512]{2,1,0:T(8,128)(2,1)} %get-tuple-element.49), channel_id=1, source_target_pairs={{0,8},{4,12},{8,0},{12,4},{1,9},{5,13},{9,1},{13,5},{2,10},{6,14},... | collective-permute-start | bytes 3145736 | tf_op jit(solution)/shard_map/ppermute | solution.py:210
  11.4 0.5 collective-permute-start.2
  11.9 0.0 copy-done.9
  11.9 0.1 copy.54
  12.0 1.1 copy.38
  13.7 0.0 copy-done.10
  13.7 0.2 convolution_minimum_fusion.5
  14.0 0.2 convolution_minimum_fusion.4
  14.1 0.2 convolution_minimum_fusion.3
  14.3 0.2 convolution_minimum_fusion.2
  14.5 0.2 convolution_minimum_fusion.1
  14.6 0.2 fusion.10
  14.8 0.7 broadcast_11_ones_ref_rest_1_.2.ones_ref.rest_1_
  15.5 57.5 %shard_map.104 = (f32[4,512,1]{2,1,0:T(8,128)}, f32[4,512,128]{2,1,0:T(8,128)}, f32[4,512,128]{2,1,0:T(8,128)}) custom-call(s32[1]{0:T(128)} %bitcast.5.nv_ref, bf16[4,512,128]{2,1,0:T(8,128)(2,1)} %bitcast.100, bf16[2,8192,512]{2,1,0:T(8,128)(2,1)} %bitcast.116, bf16[512,128]{1,0:T(8,128)(2,1)} %broadcast_11_ones_ref_rest_1_.2.ones_ref.rest_1_), custom_call_target="tpu_custom_call" | custom-call | flops 12884901888 | bytes 17301504 | tf_op jit(solution)/shard_map/pallas_call | solution.py:91
  73.0 0.0 copy-done
  73.0 0.0 copy-done.1
  73.0 0.0 copy-done.6
  73.0 0.0 copy-start.5
  73.1 1.2 copy-done.5
  74.3 7.1 %shard_map.105 = (f32[4,512,1]{2,1,0:T(8,128)S(1)}, f32[4,512,128]{2,1,0:T(8,128)S(1)}, f32[4,512,128]{2,1,0:T(8,128)S(1)}) custom-call(s32[1]{0:T(128)} %bitcast.3.flag_ref, bf16[4,512,128]{2,1,0:T(8,128)(2,1)S(1)} %bitcast.101, f32[4,512,1]{2,1,0:T(8,128)S(1)} %copy-done.5, f32[4,512,128]{2,1,0:T(8,128)} %get-tuple-element.18.l_ref, ...), custom_call_target="tpu_custom_call" | custom-call | flops 805306368 | bytes 1572864 | tf_op jit(solution)/shard_map/pallas_call | solution.py:161
  81.3 0.0 copy-start.2
  81.4 1.0 copy-done.2
  82.3 0.0 collective-permute-done.rest_0_
  82.3 4.9 %shard_map.106 = (f32[4,512,1]{2,1,0:T(8,128)S(1)}, f32[4,512,128]{2,1,0:T(8,128)S(1)}, f32[4,512,128]{2,1,0:T(8,128)S(1)}) custom-call(s32[1]{0:T(128)} %constant.18.clone.1.flag_ref, bf16[4,512,128]{2,1,0:T(8,128)(2,1)S(1)} %bitcast.102, f32[4,512,1]{2,1,0:T(8,128)S(1)} %get-tuple-element.20.m_ref, f32[4,512,128]{2,1,0:T(8,128)S(1)} %get-tuple-element.21.l_ref, ...), custom_call_target="tpu_custom_call" | custom-call | flops 805306368 | bytes 1572864 | tf_op jit(solution)/shard_map/pallas_call | solution.py:161
  87.2 0.0 copy-start.4
  87.2 1.0 copy-done.4
  88.2 0.0 collective-permute-done.1.rest_0_
  88.2 1.0 copy-done.8
  89.2 4.9 %shard_map.107 = (f32[4,512,1]{2,1,0:T(8,128)S(1)}, f32[4,512,128]{2,1,0:T(8,128)S(1)}, f32[4,512,128]{2,1,0:T(8,128)S(1)}) custom-call(s32[1]{0:T(128)} %constant.18.clone.1.flag_ref, bf16[4,512,128]{2,1,0:T(8,128)(2,1)S(1)} %bitcast.103, f32[4,512,1]{2,1,0:T(8,128)S(1)} %get-tuple-element.23.m_ref, f32[4,512,128]{2,1,0:T(8,128)S(1)} %get-tuple-element.24.l_ref, ...), custom_call_target="tpu_custom_call" | custom-call | flops 805306368 | bytes 1572864 | tf_op jit(solution)/shard_map/pallas_call | solution.py:161
  94.1 0.0 copy-start.3
  94.1 1.0 copy-done.3
  95.1 7.0 %collective-permute-done.2.rest_0_ = bf16[2,512,512]{2,1,0:T(8,128)(2,1)S(1)} collective-permute-done((bf16[2,512,512]{2,1,0:T(8,128)(2,1)}, bf16[2,512,512]{2,1,0:T(8,128)(2,1)S(1)}, u32[]{:S(2)}, u32[]{:S(2)}) %collective-permute-start.2) | collective-permute-done | bytes 1048608 | tf_op jit(solution)/shard_map/ppermute | solution.py:210
  102.2 1.0 copy-done.7
  103.1 4.8 %shard_map.108 = (f32[4,512,1]{2,1,0:T(8,128)S(1)}, f32[4,512,128]{2,1,0:T(8,128)S(1)}, f32[4,512,128]{2,1,0:T(8,128)S(1)}) custom-call(s32[1]{0:T(128)} %constant.18.clone.1.flag_ref, bf16[4,512,128]{2,1,0:T(8,128)(2,1)S(1)} %bitcast.104, f32[4,512,1]{2,1,0:T(8,128)S(1)} %get-tuple-element.26.m_ref, f32[4,512,128]{2,1,0:T(8,128)S(1)} %get-tuple-element.27.l_ref, ...), custom_call_target="tpu_custom_call" | custom-call | flops 805306368 | bytes 1572864 | tf_op jit(solution)/shard_map/pallas_call | solution.py:161
  108.0 0.3 slice_reduce_fusion
  108.3 0.1 divide_convert_fusion
  108.5 0.3 reduce.2
  108.8 0.1 reshape_squeeze.10
  108.9 0.1 maximum_bitcast_fusion
  109.0 0.1 reshape_squeeze.11
  109.1 0.1 maximum_bitcast_fusion.1
  109.2 0.1 pad_maximum_fusion
  109.3 12.1 %all_to_all.10 = bf16[32,66,128]{2,1,0:T(8,128)(2,1)S(1)} all-to-all(bf16[32,66,128]{2,1,0:T(8,128)(2,1)S(1)} %pad_maximum_fusion), channel_id=1, replica_groups=mesh['tensor'=2,'req'=4,'seq'=4] {'seq'}, dimensions={0} | all-to-all | bytes 1081344 | tf_op jit(solution)/shard_map/all_to_all | solution.py:272
  121.4 0.1 copy.69
  121.5 0.1 fusion.23
  121.6 0.1 fusion.29
  121.7 0.1 copy.44
  121.8 0.3 multiply_reduce_fusion
  122.1 0.1 fusion.16
  122.3 0.1 copy.46
  122.4 0.1 reshape.133
  122.4 8.4 %fusion.6 = bf16[8,64,1024]{2,1,0:T(8,128)(2,1)} fusion(bf16[64,1024,1]{1,0,2:T(8,128)(2,1)S(1)} %reshape.133, bf16[128,8,8,1024]{3,2,1,0:T(8,128)(2,1)} %bitcast.117), kind=kOutput, calls=%fused_computation.5 | convolution fusion | flops 1074266112 | bytes 17956864 | tf_op jit(solution)/shard_map/ik,kcj->cij/dot_general | solution.py:288
  130.9 3.7 %all-to-all-start.1 = ((bf16[8,64,1024]{2,1,0:T(8,128)(2,1)}), bf16[8,64,1024]{2,1,0:T(8,128)(2,1)S(1)}, u32[]{:S(2)}, u32[]{:S(2)}) async-start(bf16[8,64,1024]{2,1,0:T(8,128)(2,1)} %fusion.6), calls=%async_computation.1 | async-start | bytes 2097152 | tf_op jit(solution)/shard_map/all_to_all | solution.py:294
  134.6 0.1 copy.48
  134.7 0.0 copy-done.11
  134.8 0.6 gather_fusion
  135.4 0.1 broadcast_select_fusion
  135.4 0.6 copy.49
  136.1 13.8 %all-to-all-done.1 = bf16[8,64,1024]{2,1,0:T(8,128)(2,1)S(1)} async-done(((bf16[8,64,1024]{2,1,0:T(8,128)(2,1)}), bf16[8,64,1024]{2,1,0:T(8,128)(2,1)S(1)}, u32[]{:S(2)}, u32[]{:S(2)}) %all-to-all-start.1) | async-done | bytes 1048608 | tf_op jit(solution)/shard_map/all_to_all | solution.py:294
  149.9 0.8 reduce_sum.75
  (16 shorter events, 0.1 us)
Async XLA Ops:
  4.6 7.3 %copy-start.9 = (bf16[1,64,4096]{2,1,0:T(8,128)(2,1)S(1)}, bf16[1,64,4096]{2,1,0:T(8,128)(2,1)}, u32[]{:S(2)}) copy-start(bf16[1,64,4096]{2,1,0:T(8,128)(2,1)} %param.9) | copy-start | bytes 1572868
  8.4 5.3 %copy-start.10 = (s32[1,64]{1,0:T(1,128)S(1)}, s32[1,64]{1,0:T(1,128)}, u32[]{:S(2)}) copy-start(s32[1,64]{1,0:T(1,128)} %param.16) | copy-start | bytes 772
  8.4 73.9 %collective-permute-start = (bf16[2,512,512]{2,1,0:T(8,128)(2,1)}, bf16[2,512,512]{2,1,0:T(8,128)(2,1)}, u32[]{:S(2)}, u32[]{:S(2)}) collective-permute-start(bf16[2,512,512]{2,1,0:T(8,128)(2,1)} %get-tuple-element.50), channel_id=1, source_target_pairs={{0,4},{4,0},{8,12},{12,8},{1,5},{5,1},{9,13},{13,9},{2,6},{6,2},{1... | collective-permute-start | bytes 3145736 | tf_op jit(solution)/shard_map/ppermute | solution.py:210
  8.4 79.8 %collective-permute-start.1 = (bf16[2,512,512]{2,1,0:T(8,128)(2,1)}, bf16[2,512,512]{2,1,0:T(8,128)(2,1)S(1)}, u32[]{:S(2)}, u32[]{:S(2)}) collective-permute-start(bf16[2,512,512]{2,1,0:T(8,128)(2,1)} %get-tuple-element.49), channel_id=1, source_target_pairs={{0,8},{4,12},{8,0},{12,4},{1,9},{5,13},{9,1},{13,5},{2,10},{6,14},... | collective-permute-start | bytes 3145736 | tf_op jit(solution)/shard_map/ppermute | solution.py:210
  11.4 90.7 %collective-permute-start.2 = (bf16[2,512,512]{2,1,0:T(8,128)(2,1)}, bf16[2,512,512]{2,1,0:T(8,128)(2,1)S(1)}, u32[]{:S(2)}, u32[]{:S(2)}) collective-permute-start(bf16[2,512,512]{2,1,0:T(8,128)(2,1)} %get-tuple-element.48), channel_id=1, source_target_pairs={{0,12},{4,8},{8,4},{12,0},{1,13},{5,9},{9,5},{13,1},{2,14},{6,10},... | collective-permute-start | bytes 3145736 | tf_op jit(solution)/shard_map/ppermute | solution.py:210
  15.5 57.5 %copy-start = (bf16[64,4,8,128]{3,0,2,1:T(8,128)(2,1)S(1)}, bf16[64,4,8,128]{3,0,2,1:T(8,128)(2,1)}, u32[]{:S(2)}) copy-start(bf16[64,4,8,128]{3,0,2,1:T(8,128)(2,1)} %copy.38) | copy-start | bytes 1572868
  15.5 57.5 %copy-start.1 = (bf16[512,128]{1,0:T(8,128)(2,1)S(1)}, bf16[512,128]{1,0:T(8,128)(2,1)}, u32[]{:S(2)}) copy-start(bf16[512,128]{1,0:T(8,128)(2,1)} %broadcast_11_ones_ref_rest_1_.2.ones_ref.rest_1_) | copy-start | bytes 393220
  15.5 57.5 %copy-start.6 = (bf16[1,2,64,512]{3,2,1,0:T(8,128)(2,1)S(1)}, bf16[1,2,64,512]{3,2,1,0:T(8,128)(2,1)}, u32[]{:S(2)}) copy-start(bf16[1,2,64,512]{3,2,1,0:T(8,128)(2,1)} %param.10) | copy-start | bytes 393220
  73.0 1.2 copy-start.5
  81.3 1.0 copy-start.2
  87.2 1.0 copy-start.4
  88.2 1.0 copy-start.8
  94.1 1.0 copy-start.3
  102.2 1.0 copy-start.7
  130.9 3.8 %copy-start.11 = (s32[1,8]{1,0:T(1,128)S(1)}, s32[1,8]{1,0:T(1,128)}, u32[]{:S(2)}) copy-start(s32[1,8]{1,0:T(1,128)} %param.17) | copy-start | bytes 100
  130.9 19.0 %all-to-all-start.1 = ((bf16[8,64,1024]{2,1,0:T(8,128)(2,1)}), bf16[8,64,1024]{2,1,0:T(8,128)(2,1)S(1)}, u32[]{:S(2)}, u32[]{:S(2)}) async-start(bf16[8,64,1024]{2,1,0:T(8,128)(2,1)} %fusion.6), calls=%async_computation.1 | async-start | bytes 2097152 | tf_op jit(solution)/shard_map/all_to_all | solution.py:294

commit v6 on v5

--- a/solution.py
+++ b/solution.py
@@ -212,9 +212,9 @@
 
 
 def split16(x):
-    high = x.astype(jnp.bfloat16)
-    low = (x - high.astype(jnp.float32)).astype(jnp.bfloat16)
-    return high, low
+    high = lax.reduce_precision(x, exponent_bits=8, mantissa_bits=7)
+    low = (x - high).astype(jnp.bfloat16)
+    return high.astype(jnp.bfloat16), low
 
 
 def join16(high, low):

time: 151 us -> 151 us (level)
  no operation moved by 1% of the time
where the time goes in v6:
time: 151 us
  Pallas kernels  79.1 us (52%)
  waiting for transfers between devices  20.9 us (14%)
  blocking collectives  12.1 us (8%)
  local copies, waits for them, and re-layouts  10.3 us (7%)
  matrix products  9.48 us (6%)
  other arithmetic  7.54 us (5%)
  starting transfers between devices  7.18 us (5%)
  between operations  4.16 us (3%)
    pallas_call x1, Pallas kernels, own_attend(): pl.pallas_call(functools.partial(own_kernel, kv_heads, block), out_shape=...  57.5 us
    pallas_call x4, Pallas kernels, shared_attend(): pl.pallas_call(functools.partial(shared_kernel, kv_heads, n_blocks, tree...  21.6 us
    all_to_all x1, waiting for transfers between devices, shards(): pieces = lax.all_to_all(product, out_group, 0, 0, tiled=True)  13.8 us
    all_to_all x1, blocking collectives, shards(): packed = lax.all_to_all(packed, 'seq', 0, 0, tiled=True)  12.1 us
    dot_general x1, matrix products, shards(): jnp.einsum('ik,kcj->cij', attended, out_weight.reshape(out_weight.shape[0...  8.44 us
    ppermute x3, waiting for transfers between devices, exchange_shared(): received.append(lax.ppermute(sent, 'req', pairs))  7.04 us
    unnamed x26, local copies, waits for them, and re-layouts  6.94 us
    select_n x1, other arithmetic, pick_group(): picked = jnp.where(group == g, shared_cache[:, g], picked)  3.79 us
  transfers between devices with their start and end apart: 4, of which 2 were waited for; matrix products, arithmetic and copies ran while one was open for 3% of the time, Pallas kernels for 49%

profile of v6, /device:TPU:8, one launch (start us, length us, event | category | flops | bytes accessed | tf_op | source)
XLA Modules:
  0.0 150.7 jit_solution(8084736981285626850)
XLA Ops:
  0.6 1.4 fusion.29
  4.6 0.0 copy-start.9
  4.6 3.8 %fusion.14 = (bf16[2,512,512]{2,1,0:T(8,128)(2,1)}, bf16[2,512,512]{2,1,0:T(8,128)(2,1)}, bf16[2,512,512]{2,1,0:T(8,128)(2,1)}, bf16[2,512,512]{2,1,0:T(8,128)(2,1)}) fusion(pred[]{:T(512)S(6)} %eq.74, bf16[2,2,512,512]{3,2,1,0:T(8,128)(2,1)} %param.12, pred[]{:T(512)S(6)} %eq.71, pred[]{:T(512)S(6)} %eq.68, pred[]{:T(512)S(6)} %eq.60), kind=kLoop, calls=%fused_computation.21 | loop fusion | flops 2097152 | bytes 6291460 | tf_op jit(solution)/shard_map/jit(_where)/select_n | solution.py:195
  8.4 0.0 collective-permute-start
  8.4 3.0 %collective-permute-start.1 = (bf16[2,512,512]{2,1,0:T(8,128)(2,1)}, bf16[2,512,512]{2,1,0:T(8,128)(2,1)S(1)}, u32[]{:S(2)}, u32[]{:S(2)}) collective-permute-start(bf16[2,512,512]{2,1,0:T(8,128)(2,1)} %get-tuple-element.45), channel_id=1, source_target_pairs={{0,8},{4,12},{8,0},{12,4},{1,9},{5,13},{9,1},{13,5},{2,10},{6,14},... | collective-permute-start | bytes 3145736 | tf_op jit(solution)/shard_map/ppermute | solution.py:210
  11.4 0.5 collective-permute-start.2
  11.9 0.0 copy-done.9
  11.9 0.1 copy.54
  12.0 1.1 copy.38
  13.7 0.0 copy-done.10
  13.7 0.2 convolution_minimum_fusion.5
  14.0 0.2 convolution_minimum_fusion.4
  14.1 0.2 convolution_minimum_fusion.3
  14.3 0.2 convolution_minimum_fusion.2
  14.5 0.2 convolution_minimum_fusion.1
  14.6 0.2 fusion.10
  14.8 0.7 broadcast_11_ones_ref_rest_1_.2.ones_ref.rest_1_
  15.5 57.5 %shard_map.104 = (f32[4,512,1]{2,1,0:T(8,128)}, f32[4,512,128]{2,1,0:T(8,128)}, f32[4,512,128]{2,1,0:T(8,128)}) custom-call(s32[1]{0:T(128)} %bitcast.5.nv_ref, bf16[4,512,128]{2,1,0:T(8,128)(2,1)} %bitcast.100, bf16[2,8192,512]{2,1,0:T(8,128)(2,1)} %bitcast.116, bf16[512,128]{1,0:T(8,128)(2,1)} %broadcast_11_ones_ref_rest_1_.2.ones_ref.rest_1_), custom_call_target="tpu_custom_call" | custom-call | flops 12884901888 | bytes 17301504 | tf_op jit(solution)/shard_map/pallas_call | solution.py:91
  73.0 0.0 copy-done
  73.0 0.0 copy-done.1
  73.0 0.0 copy-done.6
  73.0 0.0 copy-start.5
  73.1 1.2 copy-done.5
  74.3 7.1 %shard_map.105 = (f32[4,512,1]{2,1,0:T(8,128)S(1)}, f32[4,512,128]{2,1,0:T(8,128)S(1)}, f32[4,512,128]{2,1,0:T(8,128)S(1)}) custom-call(s32[1]{0:T(128)} %bitcast.3.flag_ref, bf16[4,512,128]{2,1,0:T(8,128)(2,1)S(1)} %bitcast.101, f32[4,512,1]{2,1,0:T(8,128)S(1)} %copy-done.5, f32[4,512,128]{2,1,0:T(8,128)} %get-tuple-element.18.l_ref, ...), custom_call_target="tpu_custom_call" | custom-call | flops 805306368 | bytes 1572864 | tf_op jit(solution)/shard_map/pallas_call | solution.py:161
  81.3 0.0 copy-start.2
  81.4 1.0 copy-done.2
  82.3 0.0 collective-permute-done.rest_0_
  82.3 4.9 %shard_map.106 = (f32[4,512,1]{2,1,0:T(8,128)S(1)}, f32[4,512,128]{2,1,0:T(8,128)S(1)}, f32[4,512,128]{2,1,0:T(8,128)S(1)}) custom-call(s32[1]{0:T(128)} %constant.18.clone.1.flag_ref, bf16[4,512,128]{2,1,0:T(8,128)(2,1)S(1)} %bitcast.102, f32[4,512,1]{2,1,0:T(8,128)S(1)} %get-tuple-element.20.m_ref, f32[4,512,128]{2,1,0:T(8,128)S(1)} %get-tuple-element.21.l_ref, ...), custom_call_target="tpu_custom_call" | custom-call | flops 805306368 | bytes 1572864 | tf_op jit(solution)/shard_map/pallas_call | solution.py:161
  87.2 0.0 copy-start.4
  87.2 1.0 copy-done.4
  88.2 0.0 collective-permute-done.1.rest_0_
  88.2 1.0 copy-done.8
  89.2 4.9 %shard_map.107 = (f32[4,512,1]{2,1,0:T(8,128)S(1)}, f32[4,512,128]{2,1,0:T(8,128)S(1)}, f32[4,512,128]{2,1,0:T(8,128)S(1)}) custom-call(s32[1]{0:T(128)} %constant.18.clone.1.flag_ref, bf16[4,512,128]{2,1,0:T(8,128)(2,1)S(1)} %bitcast.103, f32[4,512,1]{2,1,0:T(8,128)S(1)} %get-tuple-element.23.m_ref, f32[4,512,128]{2,1,0:T(8,128)S(1)} %get-tuple-element.24.l_ref, ...), custom_call_target="tpu_custom_call" | custom-call | flops 805306368 | bytes 1572864 | tf_op jit(solution)/shard_map/pallas_call | solution.py:161
  94.1 0.0 copy-start.3
  94.1 1.0 copy-done.3
  95.1 7.0 %collective-permute-done.2.rest_0_ = bf16[2,512,512]{2,1,0:T(8,128)(2,1)S(1)} collective-permute-done((bf16[2,512,512]{2,1,0:T(8,128)(2,1)}, bf16[2,512,512]{2,1,0:T(8,128)(2,1)S(1)}, u32[]{:S(2)}, u32[]{:S(2)}) %collective-permute-start.2) | collective-permute-done | bytes 1048608 | tf_op jit(solution)/shard_map/ppermute | solution.py:210
  102.2 1.0 copy-done.7
  103.1 4.8 %shard_map.108 = (f32[4,512,1]{2,1,0:T(8,128)S(1)}, f32[4,512,128]{2,1,0:T(8,128)S(1)}, f32[4,512,128]{2,1,0:T(8,128)S(1)}) custom-call(s32[1]{0:T(128)} %constant.18.clone.1.flag_ref, bf16[4,512,128]{2,1,0:T(8,128)(2,1)S(1)} %bitcast.104, f32[4,512,1]{2,1,0:T(8,128)S(1)} %get-tuple-element.26.m_ref, f32[4,512,128]{2,1,0:T(8,128)S(1)} %get-tuple-element.27.l_ref, ...), custom_call_target="tpu_custom_call" | custom-call | flops 805306368 | bytes 1572864 | tf_op jit(solution)/shard_map/pallas_call | solution.py:161
  108.0 0.3 slice_reduce_fusion
  108.3 0.1 divide_convert_fusion
  108.5 0.3 reduce.2
  108.8 0.1 reshape_squeeze.10
  108.9 0.1 maximum_bitcast_fusion
  109.0 0.1 reshape_squeeze.11
  109.1 0.1 maximum_bitcast_fusion.1
  109.2 0.1 pad_maximum_fusion
  109.3 12.1 %all_to_all.10 = bf16[32,66,128]{2,1,0:T(8,128)(2,1)S(1)} all-to-all(bf16[32,66,128]{2,1,0:T(8,128)(2,1)S(1)} %pad_maximum_fusion), channel_id=1, replica_groups=mesh['tensor'=2,'req'=4,'seq'=4] {'seq'}, dimensions={0} | all-to-all | bytes 1081344 | tf_op jit(solution)/shard_map/all_to_all | solution.py:272
  121.4 0.1 copy.69
  121.5 0.1 fusion.25
  121.6 0.1 fusion.31
  121.7 0.1 copy.44
  121.8 0.3 multiply_reduce_fusion
  122.1 0.1 fusion.16
  122.3 0.1 copy.46
  122.4 0.1 reshape.133
  122.4 8.4 %fusion.6 = bf16[8,64,1024]{2,1,0:T(8,128)(2,1)} fusion(bf16[64,1024,1]{1,0,2:T(8,128)(2,1)S(1)} %reshape.133, bf16[128,8,8,1024]{3,2,1,0:T(8,128)(2,1)} %bitcast.117), kind=kOutput, calls=%fused_computation.5 | convolution fusion | flops 1074266112 | bytes 17956864 | tf_op jit(solution)/shard_map/ik,kcj->cij/dot_general | solution.py:288
  130.9 3.7 %all-to-all-start.1 = ((bf16[8,64,1024]{2,1,0:T(8,128)(2,1)}), bf16[8,64,1024]{2,1,0:T(8,128)(2,1)S(1)}, u32[]{:S(2)}, u32[]{:S(2)}) async-start(bf16[8,64,1024]{2,1,0:T(8,128)(2,1)} %fusion.6), calls=%async_computation.1 | async-start | bytes 2097152 | tf_op jit(solution)/shard_map/all_to_all | solution.py:294
  134.6 0.1 copy.48
  134.7 0.0 copy-done.11
  134.8 0.6 gather_fusion
  135.4 0.1 broadcast_select_fusion
  135.5 0.6 copy.49
  136.1 13.8 %all-to-all-done.1 = bf16[8,64,1024]{2,1,0:T(8,128)(2,1)S(1)} async-done(((bf16[8,64,1024]{2,1,0:T(8,128)(2,1)}), bf16[8,64,1024]{2,1,0:T(8,128)(2,1)S(1)}, u32[]{:S(2)}, u32[]{:S(2)}) %all-to-all-start.1) | async-done | bytes 1048608 | tf_op jit(solution)/shard_map/all_to_all | solution.py:294
  149.9 0.8 reduce_sum.75
  (16 shorter events, 0.1 us)
Async XLA Ops:
  4.6 7.3 %copy-start.9 = (bf16[1,64,4096]{2,1,0:T(8,128)(2,1)S(1)}, bf16[1,64,4096]{2,1,0:T(8,128)(2,1)}, u32[]{:S(2)}) copy-start(bf16[1,64,4096]{2,1,0:T(8,128)(2,1)} %param.9) | copy-start | bytes 1572868
  8.4 5.3 %copy-start.10 = (s32[1,64]{1,0:T(1,128)S(1)}, s32[1,64]{1,0:T(1,128)}, u32[]{:S(2)}) copy-start(s32[1,64]{1,0:T(1,128)} %param.16) | copy-start | bytes 772
  8.4 73.9 %collective-permute-start = (bf16[2,512,512]{2,1,0:T(8,128)(2,1)}, bf16[2,512,512]{2,1,0:T(8,128)(2,1)}, u32[]{:S(2)}, u32[]{:S(2)}) collective-permute-start(bf16[2,512,512]{2,1,0:T(8,128)(2,1)} %get-tuple-element.46), channel_id=1, source_target_pairs={{0,4},{4,0},{8,12},{12,8},{1,5},{5,1},{9,13},{13,9},{2,6},{6,2},{1... | collective-permute-start | bytes 3145736 | tf_op jit(solution)/shard_map/ppermute | solution.py:210
  8.4 79.8 %collective-permute-start.1 = (bf16[2,512,512]{2,1,0:T(8,128)(2,1)}, bf16[2,512,512]{2,1,0:T(8,128)(2,1)S(1)}, u32[]{:S(2)}, u32[]{:S(2)}) collective-permute-start(bf16[2,512,512]{2,1,0:T(8,128)(2,1)} %get-tuple-element.45), channel_id=1, source_target_pairs={{0,8},{4,12},{8,0},{12,4},{1,9},{5,13},{9,1},{13,5},{2,10},{6,14},... | collective-permute-start | bytes 3145736 | tf_op jit(solution)/shard_map/ppermute | solution.py:210
  11.4 90.7 %collective-permute-start.2 = (bf16[2,512,512]{2,1,0:T(8,128)(2,1)}, bf16[2,512,512]{2,1,0:T(8,128)(2,1)S(1)}, u32[]{:S(2)}, u32[]{:S(2)}) collective-permute-start(bf16[2,512,512]{2,1,0:T(8,128)(2,1)} %get-tuple-element.44), channel_id=1, source_target_pairs={{0,12},{4,8},{8,4},{12,0},{1,13},{5,9},{9,5},{13,1},{2,14},{6,10},... | collective-permute-start | bytes 3145736 | tf_op jit(solution)/shard_map/ppermute | solution.py:210
  15.5 57.5 %copy-start = (bf16[64,4,8,128]{3,0,2,1:T(8,128)(2,1)S(1)}, bf16[64,4,8,128]{3,0,2,1:T(8,128)(2,1)}, u32[]{:S(2)}) copy-start(bf16[64,4,8,128]{3,0,2,1:T(8,128)(2,1)} %copy.38) | copy-start | bytes 1572868
  15.5 57.5 %copy-start.1 = (bf16[512,128]{1,0:T(8,128)(2,1)S(1)}, bf16[512,128]{1,0:T(8,128)(2,1)}, u32[]{:S(2)}) copy-start(bf16[512,128]{1,0:T(8,128)(2,1)} %broadcast_11_ones_ref_rest_1_.2.ones_ref.rest_1_) | copy-start | bytes 393220
  15.5 57.5 %copy-start.6 = (bf16[1,2,64,512]{3,2,1,0:T(8,128)(2,1)S(1)}, bf16[1,2,64,512]{3,2,1,0:T(8,128)(2,1)}, u32[]{:S(2)}) copy-start(bf16[1,2,64,512]{3,2,1,0:T(8,128)(2,1)} %param.10) | copy-start | bytes 393220
  73.0 1.2 copy-start.5
  81.3 1.0 copy-start.2
  87.2 1.0 copy-start.4
  88.2 1.0 copy-start.8
  94.1 1.0 copy-start.3
  102.2 1.0 copy-start.7
  130.9 3.8 %copy-start.11 = (s32[1,8]{1,0:T(1,128)S(1)}, s32[1,8]{1,0:T(1,128)}, u32[]{:S(2)}) copy-start(s32[1,8]{1,0:T(1,128)} %param.17) | copy-start | bytes 100
  130.9 19.0 %all-to-all-start.1 = ((bf16[8,64,1024]{2,1,0:T(8,128)(2,1)}), bf16[8,64,1024]{2,1,0:T(8,128)(2,1)S(1)}, u32[]{:S(2)}, u32[]{:S(2)}) async-start(bf16[8,64,1024]{2,1,0:T(8,128)(2,1)} %fusion.6), calls=%async_computation.1 | async-start | bytes 2097152 | tf_op jit(solution)/shard_map/all_to_all | solution.py:294
